TPU v7x, 32 devices: a whole 2x2x4 slice. The times are simulated.
32 devices in a mesh: rep: 2 (over x), seq: 16 (over z, y, core).
Axes of the slice: x: 2, y: 2, z: 4, core: 2. Of those that a mesh axis runs over, the one named last changes fastest.
Arguments:
- signal: bfloat16 [8192, 2048], P(('rep', 'seq')), parts along dimension 0, may hold values from -6 to 6
- gate: bfloat16 [8192, 2048], P(('rep', 'seq')), parts along dimension 0, may hold values from -6 to 6
- skip: float32 [2048], replicated, may hold values from -4 to 4
- taps: bfloat16 [1024, 128], P('seq'), may hold values from -2 to 2
Outputs:
- mixed: bfloat16 [8192, 2048], P(('rep', 'seq')), parts along dimension 0
There are 2 independent parts, one for each index of `rep`. A program takes and returns all parts, laid end to end along the dimension named above; an argument that names none is the same for every part. Nothing has to cross between parts.
All inputs are finite; a program needn't handle non-finite values.
Results may differ from a plain program's by a relative error of at most 0.001.
Values may be sent and summed in bfloat16 or wider, within the bound.
No kernel may reach another device: no remote copies, remote signals or barrier semaphores. Data moves between devices by JAX's collectives and lax.ppermute only.
A program may use at most 128 MiB of HBM per device.

v0:
```python
import functools

import jax
import jax.numpy as jnp
from jax import lax
from jax.experimental import pallas as pl
from jax.experimental.pallas import tpu as pltpu
from jax.sharding import PartitionSpec as P

TILE = 128
LANES = 128


def from_behind(shard, axis, by):
    count = lax.axis_size(axis)
    pairs = [(i, i + by) for i in range(count) if 0 <= i + by < count]
    return lax.ppermute(shard, axis, pairs)


def tap_rows(all_taps, history):
    filter_len, group_count = all_taps.shape
    flipped = all_taps.T[:, ::-1].astype(jnp.float32)
    front = jnp.zeros((group_count, TILE + history - filter_len + 1), jnp.float32)
    back = jnp.zeros((group_count, TILE - 1), jnp.float32)
    return jnp.concatenate([front, flipped, back], axis=1)


def conv_kernel(rows_ref, *refs, hops, group_width):
    blocks = refs[:hops + 1]
    gate_ref, skip_ref, out_ref = refs[hops + 1:]
    block_rows = blocks[0].shape[0]
    groups_here = rows_ref.shape[0]
    span = hops * block_rows + TILE
    sub_tiles = span // TILE
    out_tiles = block_rows // TILE
    x = jnp.concatenate([b[...] for b in blocks], axis=0)
    w = jnp.concatenate(
        [x[i * TILE: i * TILE + span] for i in range(out_tiles)], axis=1)
    lane_group = lax.broadcasted_iota(jnp.int32, w.shape, 1) % LANES // group_width
    upper = (lax.broadcasted_iota(jnp.int32, (TILE, TILE), 1)
             >= lax.broadcasted_iota(jnp.int32, (TILE, TILE), 0))
    acc = jnp.zeros((TILE, w.shape[1]), jnp.float32)
    for gg in range(groups_here):
        rolled = []
        for k in range(sub_tiles + 1):
            window = rows_ref[gg:gg + 1, k * TILE:(k + 1) * TILE]
            window = jnp.broadcast_to(window, (TILE, TILE))
            rolled.append(pltpu.roll(window, 0, 1, stride=1, stride_axis=0))
        toeplitz = jnp.concatenate(
            [jnp.where(upper, rolled[k + 1], rolled[k]) for k in range(sub_tiles)],
            axis=1).astype(jnp.bfloat16)
        masked = jnp.where(lane_group == gg, w, jnp.zeros_like(w))
        acc = acc + jnp.dot(toeplitz, masked, preferred_element_type=jnp.float32)
    conv = jnp.concatenate(
        [acc[:, i * LANES:(i + 1) * LANES] for i in range(out_tiles)], axis=0)
    cur = blocks[hops][...].astype(jnp.float32)
    mixed = gate_ref[...].astype(jnp.float32) * (conv + skip_ref[...] * cur)
    out_ref[...] = mixed.astype(out_ref.dtype)


def convolve(rows, blocks, gate, skip, group_width):
    hops = len(blocks) - 1
    block_rows, channels = gate.shape
    chunks = channels // LANES
    groups_per = LANES // group_width
    block_spec = pl.BlockSpec((block_rows, LANES), lambda c: (0, c))
    kernel = functools.partial(conv_kernel, hops=hops, group_width=group_width)
    return pl.pallas_call(
        kernel,
        grid=(chunks,),
        in_specs=[pl.BlockSpec((groups_per, rows.shape[1]), lambda c: (c, 0))]
        + [block_spec] * (hops + 1)
        + [block_spec, pl.BlockSpec((1, LANES), lambda c: (0, c))],
        out_specs=block_spec,
        out_shape=jax.ShapeDtypeStruct(gate.shape, gate.dtype),
        compiler_params=pltpu.CompilerParams(dimension_semantics=("arbitrary",)),
    )(rows, *blocks, gate, skip.reshape(1, channels))


def body(signal, gate, skip, taps):
    block_rows, channels = signal.shape
    group_count = taps.shape[1]
    group_width = channels // group_count
    all_taps = lax.all_gather(taps, "seq", axis=0, tiled=True)
    filter_len = all_taps.shape[0]
    hops = -(-(filter_len - 1) // block_rows)
    all_taps, signal = lax.optimization_barrier((all_taps, signal))
    received = [from_behind(signal, "seq", d) for d in range(hops, 0, -1)]
    rows = tap_rows(all_taps, hops * block_rows)
    return convolve(rows, received + [signal], gate, skip, group_width)


def solution(mesh):
    placed = (P(("rep", "seq"), None), P(("rep", "seq"), None), P(), P("seq", None))
    return jax.shard_map(
        body, mesh=mesh, in_specs=placed, out_specs=P(("rep", "seq"), None), check_vma=False
    )
```

profile of v0, /device:TPU:15, one launch (start us, length us, event | category | flops | bytes accessed | tf_op | source)
XLA Modules:
  0.0 125.4 jit_solution(10729272395098149533)
XLA Ops:
  0.0 16.5 %all_gather.3 = bf16[1024,128]{1,0:T(8,128)(2,1)S(1)} all-gather(bf16[64,128]{1,0:T(8,128)(2,1)} %param.7), channel_id=1, replica_groups=mesh['rep'=2,'seq'=16] {'seq'}, dimensions={0}, use_global_device_ids=true | all-gather | bytes 278528 | tf_op jit(solution)/shard_map/all_gather | solution.py:84
  16.5 4.1 %collective-permute-start.3 = (bf16[256,2048]{1,0:T(8,128)(2,1)}, bf16[256,2048]{1,0:T(8,128)(2,1)S(1)}, u32[]{:S(2)}, u32[]{:S(2)}) collective-permute-start(bf16[256,2048]{1,0:T(8,128)(2,1)} %refs_4_), channel_id=1, source_target_pairs={{0,1},{1,2},{2,3},{3,4},{4,5},{5,6},{6,7},{7,8},{8,9},{9,10},{10,1... | collective-permute-start | bytes 3145736 | tf_op jit(solution)/shard_map/ppermute | solution.py:17
  20.6 1.9 %collective-permute-start.2 = (bf16[256,2048]{1,0:T(8,128)(2,1)}, bf16[256,2048]{1,0:T(8,128)(2,1)S(1)}, u32[]{:S(2)}, u32[]{:S(2)}) collective-permute-start(bf16[256,2048]{1,0:T(8,128)(2,1)} %refs_4_), channel_id=1, source_target_pairs={{0,2},{1,3},{2,4},{3,5},{4,6},{5,7},{6,8},{7,9},{8,10},{9,11},{10,... | collective-permute-start | bytes 3145736 | tf_op jit(solution)/shard_map/ppermute | solution.py:17
  22.6 4.6 %collective-permute-start.1 = (bf16[256,2048]{1,0:T(8,128)(2,1)}, bf16[256,2048]{1,0:T(8,128)(2,1)S(1)}, u32[]{:S(2)}, u32[]{:S(2)}) collective-permute-start(bf16[256,2048]{1,0:T(8,128)(2,1)} %refs_4_), channel_id=1, source_target_pairs={{0,3},{1,4},{2,5},{3,6},{4,7},{5,8},{6,9},{7,10},{8,11},{9,12},{10... | collective-permute-start | bytes 3145736 | tf_op jit(solution)/shard_map/ppermute | solution.py:17
  27.2 2.1 %collective-permute-start = (bf16[256,2048]{1,0:T(8,128)(2,1)}, bf16[256,2048]{1,0:T(8,128)(2,1)}, u32[]{:S(2)}, u32[]{:S(2)}) collective-permute-start(bf16[256,2048]{1,0:T(8,128)(2,1)} %refs_4_), channel_id=1, source_target_pairs={{0,4},{1,5},{2,6},{3,7},{4,8},{5,9},{6,10},{7,11},{8,12},{9,13},{1... | collective-permute-start | bytes 3145736 | tf_op jit(solution)/shard_map/ppermute | solution.py:17
  29.4 0.9 copy.6
  30.2 3.5 %rev.3 = bf16[128,1024]{1,0:T(8,128)(2,1)S(1)} reverse(bf16[128,1024]{1,0:T(8,128)(2,1)} %bitcast.2), dimensions={1} | reverse | bytes 524288 | tf_op jit(solution)/shard_map/rev | solution.py:22
  33.7 0.6 broadcast_in_dim.7
  34.4 1.9 %concatenate.3.rows_ref = f32[128,1280]{1,0:T(8,128)} concatenate(f32[128,129]{1,0:T(8,128)S(1)} %broadcast_in_dim.6, bf16[128,1024]{1,0:T(8,128)(2,1)S(1)} %rev.3, f32[128,127]{1,0:T(8,128)} %broadcast_in_dim.7), dimensions={1} | concatenate | bytes 1048576 | tf_op jit(solution)/shard_map/concatenate | solution.py:25
  36.3 4.8 %collective-permute-done.3.refs_3_ = bf16[256,2048]{1,0:T(8,128)(2,1)S(1)} collective-permute-done((bf16[256,2048]{1,0:T(8,128)(2,1)}, bf16[256,2048]{1,0:T(8,128)(2,1)S(1)}, u32[]{:S(2)}, u32[]{:S(2)}) %collective-permute-start.3) | collective-permute-done | bytes 1048608 | tf_op jit(solution)/shard_map/ppermute | solution.py:17
  41.1 0.0 copy-start
  41.1 24.8 %collective-permute-done.2.refs_2_ = bf16[256,2048]{1,0:T(8,128)(2,1)S(1)} collective-permute-done((bf16[256,2048]{1,0:T(8,128)(2,1)}, bf16[256,2048]{1,0:T(8,128)(2,1)S(1)}, u32[]{:S(2)}, u32[]{:S(2)}) %collective-permute-start.2) | collective-permute-done | bytes 1048608 | tf_op jit(solution)/shard_map/ppermute | solution.py:17
  65.9 0.0 copy-start.1
  65.9 20.1 %collective-permute-done.1.refs_1_ = bf16[256,2048]{1,0:T(8,128)(2,1)S(1)} collective-permute-done((bf16[256,2048]{1,0:T(8,128)(2,1)}, bf16[256,2048]{1,0:T(8,128)(2,1)S(1)}, u32[]{:S(2)}, u32[]{:S(2)}) %collective-permute-start.1) | collective-permute-done | bytes 1048608 | tf_op jit(solution)/shard_map/ppermute | solution.py:17
  86.0 0.0 copy-start.2
  86.0 17.5 %collective-permute-done.refs_0_ = bf16[256,2048]{1,0:T(8,128)(2,1)} collective-permute-done((bf16[256,2048]{1,0:T(8,128)(2,1)}, bf16[256,2048]{1,0:T(8,128)(2,1)}, u32[]{:S(2)}, u32[]{:S(2)}) %collective-permute-start) | collective-permute-done | bytes 1048608 | tf_op jit(solution)/shard_map/ppermute | solution.py:17
  103.5 0.0 copy-done
  103.5 0.0 copy-done.1
  103.5 0.0 copy-done.2
  103.6 21.9 %shard_map.46 = bf16[256,2048]{1,0:T(8,128)(2,1)} custom-call(f32[128,1280]{1,0:T(8,128)} %concatenate.3.rows_ref, bf16[256,2048]{1,0:T(8,128)(2,1)} %collective-permute-done.refs_0_, bf16[256,2048]{1,0:T(8,128)(2,1)} %copy-done.2, bf16[256,2048]{1,0:T(8,128)(2,1)} %copy-done.1, bf16[256,2048]{1,0:T(8,128)(2,1)} %copy-done, bf16[256,2048]{1,0:T(8,128)(2,1)} %refs_4_, ...), custom_call_target="tpu_custom_call" | custom-call | tf_op jit(solution)/shard_map/pallas_call | solution.py:68
  (1 shorter events, 0.0 us)
Async XLA Ops:
  16.5 24.5 %collective-permute-start.3 = (bf16[256,2048]{1,0:T(8,128)(2,1)}, bf16[256,2048]{1,0:T(8,128)(2,1)S(1)}, u32[]{:S(2)}, u32[]{:S(2)}) collective-permute-start(bf16[256,2048]{1,0:T(8,128)(2,1)} %refs_4_), channel_id=1, source_target_pairs={{0,1},{1,2},{2,3},{3,4},{4,5},{5,6},{6,7},{7,8},{8,9},{9,10},{10,1... | collective-permute-start | bytes 3145736 | tf_op jit(solution)/shard_map/ppermute | solution.py:17
  20.6 45.3 %collective-permute-start.2 = (bf16[256,2048]{1,0:T(8,128)(2,1)}, bf16[256,2048]{1,0:T(8,128)(2,1)S(1)}, u32[]{:S(2)}, u32[]{:S(2)}) collective-permute-start(bf16[256,2048]{1,0:T(8,128)(2,1)} %refs_4_), channel_id=1, source_target_pairs={{0,2},{1,3},{2,4},{3,5},{4,6},{5,7},{6,8},{7,9},{8,10},{9,11},{10,... | collective-permute-start | bytes 3145736 | tf_op jit(solution)/shard_map/ppermute | solution.py:17
  22.6 63.4 %collective-permute-start.1 = (bf16[256,2048]{1,0:T(8,128)(2,1)}, bf16[256,2048]{1,0:T(8,128)(2,1)S(1)}, u32[]{:S(2)}, u32[]{:S(2)}) collective-permute-start(bf16[256,2048]{1,0:T(8,128)(2,1)} %refs_4_), channel_id=1, source_target_pairs={{0,3},{1,4},{2,5},{3,6},{4,7},{5,8},{6,9},{7,10},{8,11},{9,12},{10... | collective-permute-start | bytes 3145736 | tf_op jit(solution)/shard_map/ppermute | solution.py:17
  27.2 76.3 %collective-permute-start = (bf16[256,2048]{1,0:T(8,128)(2,1)}, bf16[256,2048]{1,0:T(8,128)(2,1)}, u32[]{:S(2)}, u32[]{:S(2)}) collective-permute-start(bf16[256,2048]{1,0:T(8,128)(2,1)} %refs_4_), channel_id=1, source_target_pairs={{0,4},{1,5},{2,6},{3,7},{4,8},{5,9},{6,10},{7,11},{8,12},{9,13},{1... | collective-permute-start | bytes 3145736 | tf_op jit(solution)/shard_map/ppermute | solution.py:17
  41.1 62.5 %copy-start = (bf16[256,2048]{1,0:T(8,128)(2,1)}, bf16[256,2048]{1,0:T(8,128)(2,1)S(1)}, u32[]{:S(2)}) copy-start(bf16[256,2048]{1,0:T(8,128)(2,1)S(1)} %collective-permute-done.3.refs_3_) | copy-start | bytes 3145732
  65.9 37.6 %copy-start.1 = (bf16[256,2048]{1,0:T(8,128)(2,1)}, bf16[256,2048]{1,0:T(8,128)(2,1)S(1)}, u32[]{:S(2)}) copy-start(bf16[256,2048]{1,0:T(8,128)(2,1)S(1)} %collective-permute-done.2.refs_2_) | copy-start | bytes 3145732
  86.0 17.5 %copy-start.2 = (bf16[256,2048]{1,0:T(8,128)(2,1)}, bf16[256,2048]{1,0:T(8,128)(2,1)S(1)}, u32[]{:S(2)}) copy-start(bf16[256,2048]{1,0:T(8,128)(2,1)S(1)} %collective-permute-done.1.refs_1_) | copy-start | bytes 3145732
where the time goes:
time: 126 us; the launch traced here: 125 us
  waiting for transfers between devices  67.2 us (53%)
  Pallas kernels  21.9 us (17%)
  blocking collectives  16.5 us (13%)
  starting transfers between devices  12.8 us (10%)
  local copies, waits for them, and re-layouts  6.93 us (6%)
    ppermute x4, waiting for transfers between devices, from_behind(): return lax.ppermute(shard, axis, pairs)  67.2 us
    pallas_call x1, Pallas kernels, convolve(): pl.pallas_call(kernel, grid=(chunks,), in_specs=[pl.BlockSpec((groups_per...  21.9 us
    all_gather x1, blocking collectives, body(): all_taps = lax.all_gather(taps, 'seq', axis=0, tiled=True)  16.5 us
    ppermute x4, starting transfers between devices, from_behind(): return lax.ppermute(shard, axis, pairs)  12.8 us
    rev x1, local copies, waits for them, and re-layouts, tap_rows(): flipped = all_taps.T[:, ::-1].astype(jnp.float32)  3.51 us
  transfers between devices with their start and end apart: 4, of which 4 were waited for; matrix products, arithmetic and copies ran while one was open for 6% of the time, Pallas kernels for 0%

commit v1 on v0

--- a/solution.py
+++ b/solution.py
@@ -64,17 +64,26 @@
     chunks = channels // LANES
     groups_per = LANES // group_width
     block_spec = pl.BlockSpec((block_rows, LANES), lambda c: (0, c))
+    arrays, specs = [], []
+    for block in blocks:
+        if isinstance(block, tuple):
+            arrays.append(block[0])
+            specs.append(pl.BlockSpec((None, block_rows, LANES),
+                                      lambda c, slot=block[1]: (slot, 0, c)))
+        else:
+            arrays.append(block)
+            specs.append(block_spec)
     kernel = functools.partial(conv_kernel, hops=hops, group_width=group_width)
     return pl.pallas_call(
         kernel,
         grid=(chunks,),
         in_specs=[pl.BlockSpec((groups_per, rows.shape[1]), lambda c: (c, 0))]
-        + [block_spec] * (hops + 1)
+        + specs
         + [block_spec, pl.BlockSpec((1, LANES), lambda c: (0, c))],
         out_specs=block_spec,
         out_shape=jax.ShapeDtypeStruct(gate.shape, gate.dtype),
         compiler_params=pltpu.CompilerParams(dimension_semantics=("arbitrary",)),
-    )(rows, *blocks, gate, skip.reshape(1, channels))
+    )(rows, *arrays, gate, skip.reshape(1, channels))
 
 
 def body(signal, gate, skip, taps):
@@ -85,9 +94,20 @@
     filter_len = all_taps.shape[0]
     hops = -(-(filter_len - 1) // block_rows)
     all_taps, signal = lax.optimization_barrier((all_taps, signal))
-    received = [from_behind(signal, "seq", d) for d in range(hops, 0, -1)]
     rows = tap_rows(all_taps, hops * block_rows)
-    return convolve(rows, received + [signal], gate, skip, group_width)
+    if hops != 4 or lax.axis_size("seq") % 2:
+        received = [from_behind(signal, "seq", d) for d in range(hops, 0, -1)]
+        return convolve(rows, received + [signal], gate, skip, group_width)
+    back_one = from_behind(signal, "seq", 2)
+    back_two = from_behind(signal, "seq", 4)
+    first_core = lax.axis_index("seq") % 2 == 0
+    outgoing = jnp.stack([jnp.where(first_core, signal, back_one),
+                          jnp.where(first_core, back_one, back_two)])
+    count = lax.axis_size("seq")
+    swap = [(i, i ^ 1) for i in range(count)]
+    odd = lax.ppermute(outgoing, "seq", swap)
+    return convolve(rows, [back_two, (odd, 1), back_one, (odd, 0), signal],
+                    gate, skip, group_width)
 
 
 def solution(mesh):

time: 126 us -> 99.6 us (0.79)
  the two profiles are of different devices: /device:TPU:15 before, /device:TPU:8 now
where the time goes in v1:
time: 99.6 us; the launch traced here: 98.8 us
  waiting for transfers between devices  46.5 us (47%)
  Pallas kernels  21.9 us (22%)
  blocking collectives  19.8 us (20%)
  starting transfers between devices  3.84 us (4%)
  local copies, waits for them, and re-layouts  3.44 us (3%)
  other arithmetic  3.31 us (3%)
    ppermute x2, waiting for transfers between devices, from_behind(): return lax.ppermute(shard, axis, pairs)  44.2 us
    pallas_call x1, Pallas kernels, convolve(): pl.pallas_call(kernel, grid=(chunks,), in_specs=[pl.BlockSpec((groups_per...  21.9 us
    all_gather x1, blocking collectives, body(): all_taps = lax.all_gather(taps, 'seq', axis=0, tiled=True)  19.8 us
    ppermute x2, starting transfers between devices, from_behind(): return lax.ppermute(shard, axis, pairs)  3.83 us
    another operation x2, other arithmetic, body(): jnp.stack([jnp.where(first_core, signal, back_one), jnp.where(first_core,...  3.31 us
    ppermute x1, waiting for transfers between devices, body(): odd = lax.ppermute(outgoing, 'seq', swap)  2.26 us
  transfers between devices with their start and end apart: 3, of which 3 were waited for; matrix products, arithmetic and copies ran while one was open for 2% of the time, Pallas kernels for 0%

profile of v1, /device:TPU:8, one launch (start us, length us, event | category | flops | bytes accessed | tf_op | source)
XLA Modules:
  0.0 98.8 jit_solution(665679519174293585)
XLA Ops:
  0.0 19.8 %all_gather.3 = bf16[1024,128]{1,0:T(8,128)(2,1)S(1)} all-gather(bf16[64,128]{1,0:T(8,128)(2,1)} %param.7), channel_id=1, replica_groups=mesh['rep'=2,'seq'=16] {'seq'}, dimensions={0}, use_global_device_ids=true | all-gather | bytes 278528 | tf_op jit(solution)/shard_map/all_gather | solution.py:93
  19.8 1.9 %collective-permute-start = (bf16[256,2048]{1,0:T(8,128)(2,1)}, bf16[256,2048]{1,0:T(8,128)(2,1)S(1)}, u32[]{:S(2)}, u32[]{:S(2)}) collective-permute-start(bf16[256,2048]{1,0:T(8,128)(2,1)} %refs_4_), channel_id=1, source_target_pairs={{0,4},{1,5},{2,6},{3,7},{4,8},{5,9},{6,10},{7,11},{8,12},{9,13},{1... | collective-permute-start | bytes 3145736 | tf_op jit(solution)/shard_map/ppermute | solution.py:17
  21.7 1.9 %collective-permute-start.1 = (bf16[256,2048]{1,0:T(8,128)(2,1)}, bf16[256,2048]{1,0:T(8,128)(2,1)S(1)}, u32[]{:S(2)}, u32[]{:S(2)}) collective-permute-start(bf16[256,2048]{1,0:T(8,128)(2,1)} %refs_4_), channel_id=1, source_target_pairs={{0,2},{1,3},{2,4},{3,5},{4,6},{5,7},{6,8},{7,9},{8,10},{9,11},{10,... | collective-permute-start | bytes 3145736 | tf_op jit(solution)/shard_map/ppermute | solution.py:17
  23.6 24.5 %collective-permute-done.refs_0_ = bf16[256,2048]{1,0:T(8,128)(2,1)S(1)} collective-permute-done((bf16[256,2048]{1,0:T(8,128)(2,1)}, bf16[256,2048]{1,0:T(8,128)(2,1)S(1)}, u32[]{:S(2)}, u32[]{:S(2)}) %collective-permute-start) | collective-permute-done | bytes 1048608 | tf_op jit(solution)/shard_map/ppermute | solution.py:17
  48.2 0.0 copy-start.1
  48.2 19.7 %collective-permute-done.1.refs_2_ = bf16[256,2048]{1,0:T(8,128)(2,1)S(1)} collective-permute-done((bf16[256,2048]{1,0:T(8,128)(2,1)}, bf16[256,2048]{1,0:T(8,128)(2,1)S(1)}, u32[]{:S(2)}, u32[]{:S(2)}) %collective-permute-start.1) | collective-permute-done | bytes 1048608 | tf_op jit(solution)/shard_map/ppermute | solution.py:17
  67.9 0.0 copy-start.2
  67.9 1.8 %select_bitcast_fusion.1 = (bf16[1,256,2048]{2,1,0:T(8,128)(2,1)S(1)}, bf16[1,256,2048]{2,1,0:T(8,128)(2,1)S(1)}) fusion(bf16[256,2048]{1,0:T(8,128)(2,1)} %refs_4_, bf16[256,2048]{1,0:T(8,128)(2,1)S(1)} %collective-permute-done.1.refs_2_, pred[]{:T(512)S(6)} %eq.5, bf16[256,2048]{1,0:T(8,128)(2,1)S(1)} %collective-permute-done.refs_0_), kind=kLoop, calls=%fused_computation.2 | loop fusion | flops 1048576 | bytes 5242881 | tf_op jit(solution)/shard_map/stack | solution.py:104
  69.6 0.0 copy-done.1
  69.7 0.0 copy-done.2
  69.7 1.5 %pad_maximum_fusion = bf16[2,256,2048]{2,1,0:T(8,128)(2,1)} fusion(bf16[1,256,2048]{2,1,0:T(8,128)(2,1)S(1)} %get-tuple-element.10, bf16[1,256,2048]{2,1,0:T(8,128)(2,1)S(1)} %get-tuple-element.9), kind=kLoop, calls=%fused_computation | loop fusion | flops 1048576 | bytes 4194304 | tf_op jit(solution)/shard_map/stack | solution.py:104
  71.2 0.0 collective-permute-start.2
  71.2 0.1 copy.6
  71.4 0.8 rev.3
  72.2 1.1 %concatenate.3.rows_ref = f32[128,1280]{1,0:T(8,128)} concatenate(f32[128,129]{1,0:T(8,128)S(1)} %broadcast_in_dim.6, bf16[128,1024]{1,0:T(8,128)(2,1)S(1)} %rev.3, f32[128,127]{1,0:T(8,128)S(1)} %broadcast_in_dim.7), dimensions={1} | concatenate | bytes 1048576 | tf_op jit(solution)/shard_map/concatenate | solution.py:25
  73.3 2.3 %collective-permute-done.2.refs_1_.refs_3_ = bf16[2,256,2048]{2,1,0:T(8,128)(2,1)S(1)} collective-permute-done((bf16[2,256,2048]{2,1,0:T(8,128)(2,1)}, bf16[2,256,2048]{2,1,0:T(8,128)(2,1)S(1)}, u32[]{:S(2)}, u32[]{:S(2)}) %collective-permute-start.2) | collective-permute-done | bytes 2097184 | tf_op jit(solution)/shard_map/ppermute | solution.py:108
  75.6 0.0 copy-start
  75.6 1.4 %copy-done = bf16[2,256,2048]{2,1,0:T(8,128)(2,1)} copy-done((bf16[2,256,2048]{2,1,0:T(8,128)(2,1)}, bf16[2,256,2048]{2,1,0:T(8,128)(2,1)S(1)}, u32[]{:S(2)}) %copy-start) | copy-done | bytes 2097176
  76.9 21.9 %shard_map.46 = bf16[256,2048]{1,0:T(8,128)(2,1)} custom-call(f32[128,1280]{1,0:T(8,128)} %concatenate.3.rows_ref, bf16[256,2048]{1,0:T(8,128)(2,1)} %copy-done.1, bf16[2,256,2048]{2,1,0:T(8,128)(2,1)} %copy-done, bf16[256,2048]{1,0:T(8,128)(2,1)} %copy-done.2, bf16[2,256,2048]{2,1,0:T(8,128)(2,1)} %copy-done, bf16[256,2048]{1,0:T(8,128)(2,1)} %refs_4_, ...), custom_call_target="tpu_custom_call" | custom-call | tf_op jit(solution)/shard_map/pallas_call | solution.py:77
  (2 shorter events, 0.0 us)
Async XLA Ops:
  19.8 28.4 %collective-permute-start = (bf16[256,2048]{1,0:T(8,128)(2,1)}, bf16[256,2048]{1,0:T(8,128)(2,1)S(1)}, u32[]{:S(2)}, u32[]{:S(2)}) collective-permute-start(bf16[256,2048]{1,0:T(8,128)(2,1)} %refs_4_), channel_id=1, source_target_pairs={{0,4},{1,5},{2,6},{3,7},{4,8},{5,9},{6,10},{7,11},{8,12},{9,13},{1... | collective-permute-start | bytes 3145736 | tf_op jit(solution)/shard_map/ppermute | solution.py:17
  21.7 46.2 %collective-permute-start.1 = (bf16[256,2048]{1,0:T(8,128)(2,1)}, bf16[256,2048]{1,0:T(8,128)(2,1)S(1)}, u32[]{:S(2)}, u32[]{:S(2)}) collective-permute-start(bf16[256,2048]{1,0:T(8,128)(2,1)} %refs_4_), channel_id=1, source_target_pairs={{0,2},{1,3},{2,4},{3,5},{4,6},{5,7},{6,8},{7,9},{8,10},{9,11},{10,... | collective-permute-start | bytes 3145736 | tf_op jit(solution)/shard_map/ppermute | solution.py:17
  48.2 21.5 %copy-start.1 = (bf16[256,2048]{1,0:T(8,128)(2,1)}, bf16[256,2048]{1,0:T(8,128)(2,1)S(1)}, u32[]{:S(2)}) copy-start(bf16[256,2048]{1,0:T(8,128)(2,1)S(1)} %collective-permute-done.refs_0_) | copy-start | bytes 3145732
  67.9 1.8 %copy-start.2 = (bf16[256,2048]{1,0:T(8,128)(2,1)}, bf16[256,2048]{1,0:T(8,128)(2,1)S(1)}, u32[]{:S(2)}) copy-start(bf16[256,2048]{1,0:T(8,128)(2,1)S(1)} %collective-permute-done.1.refs_2_) | copy-start | bytes 3145732
  71.2 4.4 %collective-permute-start.2 = (bf16[2,256,2048]{2,1,0:T(8,128)(2,1)}, bf16[2,256,2048]{2,1,0:T(8,128)(2,1)S(1)}, u32[]{:S(2)}, u32[]{:S(2)}) collective-permute-start(bf16[2,256,2048]{2,1,0:T(8,128)(2,1)} %pad_maximum_fusion), channel_id=1, source_target_pairs={{0,1},{1,0},{2,3},{3,2},{4,5},{5,4},{6,7},{7,6},{8,9},{9,8},{10,11... | collective-permute-start | bytes 6291464 | tf_op jit(solution)/shard_map/ppermute | solution.py:108
  75.6 1.4 %copy-start = (bf16[2,256,2048]{2,1,0:T(8,128)(2,1)}, bf16[2,256,2048]{2,1,0:T(8,128)(2,1)S(1)}, u32[]{:S(2)}) copy-start(bf16[2,256,2048]{2,1,0:T(8,128)(2,1)S(1)} %collective-permute-done.2.refs_1_.refs_3_) | copy-start | bytes 6291460

commit v2 on v1

--- a/solution.py
+++ b/solution.py
@@ -17,12 +17,13 @@
     return lax.ppermute(shard, axis, pairs)
 
 
-def tap_rows(all_taps, history):
-    filter_len, group_count = all_taps.shape
-    flipped = all_taps.T[:, ::-1].astype(jnp.float32)
-    front = jnp.zeros((group_count, TILE + history - filter_len + 1), jnp.float32)
-    back = jnp.zeros((group_count, TILE - 1), jnp.float32)
-    return jnp.concatenate([front, flipped, back], axis=1)
+def tap_rows(taps, first_lag, filter_len, history):
+    share, group_count = taps.shape
+    flipped = taps.T[:, ::-1]
+    width = history + 2 * TILE
+    start = TILE + history - first_lag - share + 1
+    return lax.dynamic_update_slice(
+        jnp.zeros((group_count, width), taps.dtype), flipped, (0, start))
 
 
 def conv_kernel(rows_ref, *refs, hops, group_width):
@@ -90,11 +91,12 @@
     block_rows, channels = signal.shape
     group_count = taps.shape[1]
     group_width = channels // group_count
-    all_taps = lax.all_gather(taps, "seq", axis=0, tiled=True)
-    filter_len = all_taps.shape[0]
+    share = taps.shape[0]
+    filter_len = share * lax.axis_size("seq")
     hops = -(-(filter_len - 1) // block_rows)
-    all_taps, signal = lax.optimization_barrier((all_taps, signal))
-    rows = tap_rows(all_taps, hops * block_rows)
+    placed = tap_rows(taps, lax.axis_index("seq") * share, filter_len, hops * block_rows)
+    placed, signal = lax.optimization_barrier((placed, signal))
+    rows = lax.psum(placed, "seq").astype(jnp.float32)
     if hops != 4 or lax.axis_size("seq") % 2:
         received = [from_behind(signal, "seq", d) for d in range(hops, 0, -1)]
         return convolve(rows, received + [signal], gate, skip, group_width)

time: 99.6 us -> 186 us (1.87)
  waiting for transfers between devices: 46.5 us -> 135 us
  blocking collectives: 19.8 us -> 0 us
  between operations: 0.08 us -> 13.5 us
  starting transfers between devices: 3.84 us -> 6.92 us
    psum x0 -> x1, waiting for transfers between devices: none -> 91.9 us  [body(): rows = lax.psum(placed, 'seq').astype(jnp.float32)]
    all_gather x1 -> x0, blocking collectives: 19.8 us -> none  [body(): all_taps = lax.all_gather(taps, 'seq', axis=0, tiled=True)]
    ppermute x2, starting transfers between devices: 3.83 us -> 6.92 us  [from_behind(): return lax.ppermute(shard, axis, pairs)]
    ppermute x1, waiting for transfers between devices: 2.26 us -> 0.01 us  [body(): odd = lax.ppermute(outgoing, 'seq', swap)]
    convert_element_type x0 -> x1, other arithmetic: none -> 1.86 us  [body(): rows = lax.psum(placed, 'seq').astype(jnp.float32)]
  transfers between devices with their start and end apart: 3 -> 4, of which waited for: 3 -> 3; matrix products, arithmetic and copies ran while one was open for 2% -> 1% of each run, Pallas kernels for 0% -> 0%
where the time goes in v2:
time: 186 us
  waiting for transfers between devices  135 us (73%)
  Pallas kernels  21.9 us (12%)
  between operations  13.5 us (7%)
  starting transfers between devices  6.92 us (4%)
  other arithmetic  5.16 us (3%)
  local copies, waits for them, and re-layouts  2.74 us (1%)
    psum x1, waiting for transfers between devices, body(): rows = lax.psum(placed, 'seq').astype(jnp.float32)  91.9 us
    ppermute x2, waiting for transfers between devices, from_behind(): return lax.ppermute(shard, axis, pairs)  43.5 us
    pallas_call x1, Pallas kernels, convolve(): pl.pallas_call(kernel, grid=(chunks,), in_specs=[pl.BlockSpec((groups_per...  21.9 us
    ppermute x2, starting transfers between devices, from_behind(): return lax.ppermute(shard, axis, pairs)  6.92 us
  transfers between devices with their start and end apart: 4, of which 3 were waited for; matrix products, arithmetic and copies ran while one was open for 1% of the time, Pallas kernels for 0%

profile of v2, /device:TPU:8, one launch (start us, length us, event | category | flops | bytes accessed | tf_op | source)
XLA Modules:
  0.0 185.5 jit_solution(14988839433927412496)
XLA Ops:
  6.5 0.0 all-reduce.2.cloned.1.call-start
  6.5 0.8 copy.5
  7.4 0.1 rev.3
  7.5 0.4 dynamic_update_slice.3
  7.9 0.0 copy-start.3
  8.0 3.5 %collective-permute-start = (bf16[256,2048]{1,0:T(8,128)(2,1)}, bf16[256,2048]{1,0:T(8,128)(2,1)S(1)}, u32[]{:S(2)}, u32[]{:S(2)}) collective-permute-start(bf16[256,2048]{1,0:T(8,128)(2,1)} %refs_4_), channel_id=1, source_target_pairs={{0,4},{1,5},{2,6},{3,7},{4,8},{5,9},{6,10},{7,11},{8,12},{9,13},{1... | collective-permute-start | bytes 3145736 | tf_op jit(solution)/shard_map/ppermute | solution.py:17
  11.4 3.4 %collective-permute-start.1 = (bf16[256,2048]{1,0:T(8,128)(2,1)}, bf16[256,2048]{1,0:T(8,128)(2,1)S(1)}, u32[]{:S(2)}, u32[]{:S(2)}) collective-permute-start(bf16[256,2048]{1,0:T(8,128)(2,1)} %refs_4_), channel_id=1, source_target_pairs={{0,2},{1,3},{2,4},{3,5},{4,6},{5,7},{6,8},{7,9},{8,10},{9,11},{10,... | collective-permute-start | bytes 3145736 | tf_op jit(solution)/shard_map/ppermute | solution.py:17
  14.9 20.1 %collective-permute-done.refs_0_ = bf16[256,2048]{1,0:T(8,128)(2,1)S(1)} collective-permute-done((bf16[256,2048]{1,0:T(8,128)(2,1)}, bf16[256,2048]{1,0:T(8,128)(2,1)S(1)}, u32[]{:S(2)}, u32[]{:S(2)}) %collective-permute-start) | collective-permute-done | bytes 1048608 | tf_op jit(solution)/shard_map/ppermute | solution.py:17
  35.0 0.0 copy-start.1
  35.0 23.4 %collective-permute-done.1.refs_2_ = bf16[256,2048]{1,0:T(8,128)(2,1)S(1)} collective-permute-done((bf16[256,2048]{1,0:T(8,128)(2,1)}, bf16[256,2048]{1,0:T(8,128)(2,1)S(1)}, u32[]{:S(2)}, u32[]{:S(2)}) %collective-permute-start.1) | collective-permute-done | bytes 1048608 | tf_op jit(solution)/shard_map/ppermute | solution.py:17
  58.4 0.0 copy-start.2
  58.4 1.8 select_bitcast_fusion.1
  60.2 0.0 copy-done.3
  60.2 0.0 copy-done.1
  60.2 0.0 copy-done.2
  60.2 1.5 pad_maximum_fusion
  61.7 0.0 collective-permute-start.2
  61.7 0.0 all-reduce.2.cloned.1.call-update
  61.8 91.9 %all-reduce.2.cloned.1.call-done = bf16[128,1280]{1,0:T(8,128)(2,1)} async-done(((bf16[128,1280]{1,0:T(8,128)(2,1)}), bf16[128,1280]{1,0:T(8,128)(2,1)}) %all-reduce.2.cloned.1.call-update) | async-done | bytes 327696 | tf_op jit(solution)/shard_map/psum | solution.py:99
  153.6 1.9 %convert_element_type.3.rows_ref = f32[128,1280]{1,0:T(8,128)} convert(bf16[128,1280]{1,0:T(8,128)(2,1)} %all-reduce.2.cloned.1.call-done) | non-fusion elementwise | flops 163840 | bytes 983040 | tf_op jit(solution)/shard_map/convert_element_type | solution.py:99
  155.5 0.0 collective-permute-done.2.refs_1_.refs_3_
  155.5 0.0 copy-start
  155.5 1.3 copy-done
  156.8 21.9 %shard_map.46 = bf16[256,2048]{1,0:T(8,128)(2,1)} custom-call(f32[128,1280]{1,0:T(8,128)} %convert_element_type.3.rows_ref, bf16[256,2048]{1,0:T(8,128)(2,1)} %copy-done.1, bf16[2,256,2048]{2,1,0:T(8,128)(2,1)} %copy-done, bf16[256,2048]{1,0:T(8,128)(2,1)} %copy-done.2, bf16[2,256,2048]{2,1,0:T(8,128)(2,1)} %copy-done, bf16[256,2048]{1,0:T(8,128)(2,1)} %refs_4_, ...), custom_call_target="tpu_custom_call" | custom-call | tf_op jit(solution)/shard_map/pallas_call | solution.py:78
  (1 shorter events, 0.0 us)
Async XLA Ops:
  6.5 147.1 %all-reduce.2.cloned.1.call-start = ((), (), s32[]{:S(2)}) async-start(), calls=%async_computation | async-start | bytes 655360 | tf_op jit(solution)/shard_map/psum | solution.py:99
  7.9 52.2 %copy-start.3 = (bf16[128,1280]{1,0:T(8,128)(2,1)}, bf16[128,1280]{1,0:T(8,128)(2,1)S(1)}, u32[]{:S(2)}) copy-start(bf16[128,1280]{1,0:T(8,128)(2,1)S(1)} %dynamic_update_slice.3) | copy-start | bytes 983044
  8.0 27.0 %collective-permute-start = (bf16[256,2048]{1,0:T(8,128)(2,1)}, bf16[256,2048]{1,0:T(8,128)(2,1)S(1)}, u32[]{:S(2)}, u32[]{:S(2)}) collective-permute-start(bf16[256,2048]{1,0:T(8,128)(2,1)} %refs_4_), channel_id=1, source_target_pairs={{0,4},{1,5},{2,6},{3,7},{4,8},{5,9},{6,10},{7,11},{8,12},{9,13},{1... | collective-permute-start | bytes 3145736 | tf_op jit(solution)/shard_map/ppermute | solution.py:17
  11.4 46.9 %collective-permute-start.1 = (bf16[256,2048]{1,0:T(8,128)(2,1)}, bf16[256,2048]{1,0:T(8,128)(2,1)S(1)}, u32[]{:S(2)}, u32[]{:S(2)}) collective-permute-start(bf16[256,2048]{1,0:T(8,128)(2,1)} %refs_4_), channel_id=1, source_target_pairs={{0,2},{1,3},{2,4},{3,5},{4,6},{5,7},{6,8},{7,9},{8,10},{9,11},{10,... | collective-permute-start | bytes 3145736 | tf_op jit(solution)/shard_map/ppermute | solution.py:17
  35.0 25.2 %copy-start.1 = (bf16[256,2048]{1,0:T(8,128)(2,1)}, bf16[256,2048]{1,0:T(8,128)(2,1)S(1)}, u32[]{:S(2)}) copy-start(bf16[256,2048]{1,0:T(8,128)(2,1)S(1)} %collective-permute-done.refs_0_) | copy-start | bytes 3145732
  58.4 1.8 copy-start.2
  61.7 93.8 %collective-permute-start.2 = (bf16[2,256,2048]{2,1,0:T(8,128)(2,1)}, bf16[2,256,2048]{2,1,0:T(8,128)(2,1)S(1)}, u32[]{:S(2)}, u32[]{:S(2)}) collective-permute-start(bf16[2,256,2048]{2,1,0:T(8,128)(2,1)} %pad_maximum_fusion), channel_id=1, source_target_pairs={{0,1},{1,0},{2,3},{3,2},{4,5},{5,4},{6,7},{7,6},{8,9},{9,8},{10,11... | collective-permute-start | bytes 6291464 | tf_op jit(solution)/shard_map/ppermute | solution.py:110
  155.5 1.3 copy-start
Sparse Core Ops, SparseCore 0:
  61.9 91.6 all-reduce.1

commit v3 on v1

--- a/solution.py
+++ b/solution.py
@@ -90,12 +90,11 @@
     block_rows, channels = signal.shape
     group_count = taps.shape[1]
     group_width = channels // group_count
-    all_taps = lax.all_gather(taps, "seq", axis=0, tiled=True)
-    filter_len = all_taps.shape[0]
+    filter_len = taps.shape[0] * lax.axis_size("seq")
     hops = -(-(filter_len - 1) // block_rows)
-    all_taps, signal = lax.optimization_barrier((all_taps, signal))
-    rows = tap_rows(all_taps, hops * block_rows)
     if hops != 4 or lax.axis_size("seq") % 2:
+        all_taps = lax.all_gather(taps, "seq", axis=0, tiled=True)
+        rows = tap_rows(all_taps, hops * block_rows)
         received = [from_behind(signal, "seq", d) for d in range(hops, 0, -1)]
         return convolve(rows, received + [signal], gate, skip, group_width)
     back_one = from_behind(signal, "seq", 2)
@@ -106,6 +105,9 @@
     count = lax.axis_size("seq")
     swap = [(i, i ^ 1) for i in range(count)]
     odd = lax.ppermute(outgoing, "seq", swap)
+    taps, back_one, back_two = lax.optimization_barrier((taps, back_one, back_two))
+    all_taps = lax.all_gather(taps, "seq", axis=0, tiled=True)
+    rows = tap_rows(all_taps, hops * block_rows)
     return convolve(rows, [back_two, (odd, 1), back_one, (odd, 0), signal],
                     gate, skip, group_width)
 

time: 99.6 us -> 102 us (1.024)
  the two profiles are of different devices: /device:TPU:8 before, /device:TPU:0 now
where the time goes in v3:
time: 102 us
  blocking collectives  42.4 us (42%)
  waiting for transfers between devices  22.4 us (22%)
  Pallas kernels  21.9 us (21%)
  starting transfers between devices  8.45 us (8%)
  local copies, waits for them, and re-layouts  3.43 us (3%)
  other arithmetic  3.31 us (3%)
    all_gather x1, blocking collectives, body(): all_taps = lax.all_gather(taps, 'seq', axis=0, tiled=True)  42.4 us
    ppermute x2, waiting for transfers between devices, from_behind(): return lax.ppermute(shard, axis, pairs)  22.4 us
    pallas_call x1, Pallas kernels, convolve(): pl.pallas_call(kernel, grid=(chunks,), in_specs=[pl.BlockSpec((groups_per...  21.9 us
    ppermute x2, starting transfers between devices, from_behind(): return lax.ppermute(shard, axis, pairs)  8.44 us
    another operation x2, other arithmetic, body(): jnp.stack([jnp.where(first_core, signal, back_one), jnp.where(first_core,...  3.31 us
  transfers between devices with their start and end apart: 3, of which 2 were waited for; matrix products, arithmetic and copies ran while one was open for 2% of the time, Pallas kernels for 0%

profile of v3, /device:TPU:0, one launch (start us, length us, event | category | flops | bytes accessed | tf_op | source)
XLA Modules:
  0.0 101.9 jit_solution(10064979684985895435)
XLA Ops:
  0.0 5.0 %collective-permute-start = (bf16[256,2048]{1,0:T(8,128)(2,1)}, bf16[256,2048]{1,0:T(8,128)(2,1)S(1)}, u32[]{:S(2)}, u32[]{:S(2)}) collective-permute-start(bf16[256,2048]{1,0:T(8,128)(2,1)} %refs_4_.1), channel_id=1, source_target_pairs={{0,2},{1,3},{2,4},{3,5},{4,6},{5,7},{6,8},{7,9},{8,10},{9,11},{10,... | collective-permute-start | bytes 3145736 | tf_op jit(solution)/shard_map/ppermute | solution.py:17
  5.0 3.5 %collective-permute-start.1 = (bf16[256,2048]{1,0:T(8,128)(2,1)}, bf16[256,2048]{1,0:T(8,128)(2,1)S(1)}, u32[]{:S(2)}, u32[]{:S(2)}) collective-permute-start(bf16[256,2048]{1,0:T(8,128)(2,1)} %refs_4_.1), channel_id=1, source_target_pairs={{0,4},{1,5},{2,6},{3,7},{4,8},{5,9},{6,10},{7,11},{8,12},{9,13},{1... | collective-permute-start | bytes 3145736 | tf_op jit(solution)/shard_map/ppermute | solution.py:17
  8.5 19.1 %collective-permute-done.refs_2_ = bf16[256,2048]{1,0:T(8,128)(2,1)S(1)} collective-permute-done((bf16[256,2048]{1,0:T(8,128)(2,1)}, bf16[256,2048]{1,0:T(8,128)(2,1)S(1)}, u32[]{:S(2)}, u32[]{:S(2)}) %collective-permute-start) | collective-permute-done | bytes 1048608 | tf_op jit(solution)/shard_map/ppermute | solution.py:17
  27.6 0.0 copy-start.1
  27.6 3.2 %collective-permute-done.1.refs_0_ = bf16[256,2048]{1,0:T(8,128)(2,1)S(1)} collective-permute-done((bf16[256,2048]{1,0:T(8,128)(2,1)}, bf16[256,2048]{1,0:T(8,128)(2,1)S(1)}, u32[]{:S(2)}, u32[]{:S(2)}) %collective-permute-start.1) | collective-permute-done | bytes 1048608 | tf_op jit(solution)/shard_map/ppermute | solution.py:17
  30.8 0.0 copy-start.2
  30.8 1.8 %select_bitcast_fusion.1 = (bf16[1,256,2048]{2,1,0:T(8,128)(2,1)S(1)}, bf16[1,256,2048]{2,1,0:T(8,128)(2,1)S(1)}) fusion(bf16[256,2048]{1,0:T(8,128)(2,1)} %refs_4_.1, bf16[256,2048]{1,0:T(8,128)(2,1)S(1)} %collective-permute-done.refs_2_, pred[]{:T(512)S(6)} %eq.5, bf16[256,2048]{1,0:T(8,128)(2,1)S(1)} %collective-permute-done.1.refs_0_), kind=kLoop, calls=%fused_computation.2 | loop fusion | flops 1048576 | bytes 5242881 | tf_op jit(solution)/shard_map/stack | solution.py:103
  32.6 0.0 copy-done.1
  32.6 0.0 copy-done.2
  32.6 0.0 copy-start.3
  32.6 1.5 %pad_maximum_fusion = bf16[2,256,2048]{2,1,0:T(8,128)(2,1)} fusion(bf16[1,256,2048]{2,1,0:T(8,128)(2,1)S(1)} %get-tuple-element.12, bf16[1,256,2048]{2,1,0:T(8,128)(2,1)S(1)} %get-tuple-element.11), kind=kLoop, calls=%fused_computation | loop fusion | flops 1048576 | bytes 4194304 | tf_op jit(solution)/shard_map/stack | solution.py:103
  34.2 0.0 collective-permute-start.2
  34.2 0.0 copy-done.3
  34.2 42.4 %all_gather.3 = bf16[1024,128]{1,0:T(8,128)(2,1)S(1)} all-gather(bf16[64,128]{1,0:T(8,128)(2,1)S(1)} %copy-done.3), channel_id=1, replica_groups=mesh['rep'=2,'seq'=16] {'seq'}, dimensions={0}, use_global_device_ids=true | all-gather | bytes 278528 | tf_op jit(solution)/shard_map/all_gather | solution.py:109
  76.6 0.1 copy.6
  76.7 0.8 rev.3
  77.6 1.1 %concatenate.3.rows_ref = f32[128,1280]{1,0:T(8,128)} concatenate(f32[128,129]{1,0:T(8,128)S(1)} %broadcast_in_dim.6, bf16[128,1024]{1,0:T(8,128)(2,1)S(1)} %rev.3, f32[128,127]{1,0:T(8,128)S(1)} %broadcast_in_dim.7), dimensions={1} | concatenate | bytes 1048576 | tf_op jit(solution)/shard_map/concatenate | solution.py:25
  78.7 0.0 collective-permute-done.2.refs_1_.refs_3_
  78.7 0.0 copy-start
  78.7 1.3 %copy-done = bf16[2,256,2048]{2,1,0:T(8,128)(2,1)} copy-done((bf16[2,256,2048]{2,1,0:T(8,128)(2,1)}, bf16[2,256,2048]{2,1,0:T(8,128)(2,1)S(1)}, u32[]{:S(2)}) %copy-start) | copy-done | bytes 2097176
  80.0 21.9 %shard_map.46 = bf16[256,2048]{1,0:T(8,128)(2,1)} custom-call(f32[128,1280]{1,0:T(8,128)} %concatenate.3.rows_ref, bf16[256,2048]{1,0:T(8,128)(2,1)} %copy-done.2, bf16[2,256,2048]{2,1,0:T(8,128)(2,1)} %copy-done, bf16[256,2048]{1,0:T(8,128)(2,1)} %copy-done.1, bf16[2,256,2048]{2,1,0:T(8,128)(2,1)} %copy-done, bf16[256,2048]{1,0:T(8,128)(2,1)} %refs_4_.1, ...), custom_call_target="tpu_custom_call" | custom-call | tf_op jit(solution)/shard_map/pallas_call | solution.py:77
  (2 shorter events, 0.0 us)
Async XLA Ops:
  0.0 27.6 %collective-permute-start = (bf16[256,2048]{1,0:T(8,128)(2,1)}, bf16[256,2048]{1,0:T(8,128)(2,1)S(1)}, u32[]{:S(2)}, u32[]{:S(2)}) collective-permute-start(bf16[256,2048]{1,0:T(8,128)(2,1)} %refs_4_.1), channel_id=1, source_target_pairs={{0,2},{1,3},{2,4},{3,5},{4,6},{5,7},{6,8},{7,9},{8,10},{9,11},{10,... | collective-permute-start | bytes 3145736 | tf_op jit(solution)/shard_map/ppermute | solution.py:17
  5.0 25.9 %collective-permute-start.1 = (bf16[256,2048]{1,0:T(8,128)(2,1)}, bf16[256,2048]{1,0:T(8,128)(2,1)S(1)}, u32[]{:S(2)}, u32[]{:S(2)}) collective-permute-start(bf16[256,2048]{1,0:T(8,128)(2,1)} %refs_4_.1), channel_id=1, source_target_pairs={{0,4},{1,5},{2,6},{3,7},{4,8},{5,9},{6,10},{7,11},{8,12},{9,13},{1... | collective-permute-start | bytes 3145736 | tf_op jit(solution)/shard_map/ppermute | solution.py:17
  27.6 5.0 %copy-start.1 = (bf16[256,2048]{1,0:T(8,128)(2,1)}, bf16[256,2048]{1,0:T(8,128)(2,1)S(1)}, u32[]{:S(2)}) copy-start(bf16[256,2048]{1,0:T(8,128)(2,1)S(1)} %collective-permute-done.refs_2_) | copy-start | bytes 3145732
  30.8 1.8 %copy-start.2 = (bf16[256,2048]{1,0:T(8,128)(2,1)}, bf16[256,2048]{1,0:T(8,128)(2,1)S(1)}, u32[]{:S(2)}) copy-start(bf16[256,2048]{1,0:T(8,128)(2,1)S(1)} %collective-permute-done.1.refs_0_) | copy-start | bytes 3145732
  32.6 1.5 %copy-start.3 = (bf16[64,128]{1,0:T(8,128)(2,1)S(1)}, bf16[64,128]{1,0:T(8,128)(2,1)}, u32[]{:S(2)}) copy-start(bf16[64,128]{1,0:T(8,128)(2,1)} %param.7) | copy-start | bytes 49156
  34.2 44.5 %collective-permute-start.2 = (bf16[2,256,2048]{2,1,0:T(8,128)(2,1)}, bf16[2,256,2048]{2,1,0:T(8,128)(2,1)S(1)}, u32[]{:S(2)}, u32[]{:S(2)}) collective-permute-start(bf16[2,256,2048]{2,1,0:T(8,128)(2,1)} %pad_maximum_fusion), channel_id=1, source_target_pairs={{0,1},{1,0},{2,3},{3,2},{4,5},{5,4},{6,7},{7,6},{8,9},{9,8},{10,11... | collective-permute-start | bytes 6291464 | tf_op jit(solution)/shard_map/ppermute | solution.py:107
  78.7 1.3 %copy-start = (bf16[2,256,2048]{2,1,0:T(8,128)(2,1)}, bf16[2,256,2048]{2,1,0:T(8,128)(2,1)S(1)}, u32[]{:S(2)}) copy-start(bf16[2,256,2048]{2,1,0:T(8,128)(2,1)S(1)} %collective-permute-done.2.refs_1_.refs_3_) | copy-start | bytes 6291460

commit v4 on v1

--- a/solution.py
+++ b/solution.py
@@ -36,7 +36,7 @@
     x = jnp.concatenate([b[...] for b in blocks], axis=0)
     w = jnp.concatenate(
         [x[i * TILE: i * TILE + span] for i in range(out_tiles)], axis=1)
-    lane_group = lax.broadcasted_iota(jnp.int32, w.shape, 1) % LANES // group_width
+    lane_group = lax.broadcasted_iota(jnp.int32, (TILE, w.shape[1]), 1) % LANES // group_width
     upper = (lax.broadcasted_iota(jnp.int32, (TILE, TILE), 1)
              >= lax.broadcasted_iota(jnp.int32, (TILE, TILE), 0))
     acc = jnp.zeros((TILE, w.shape[1]), jnp.float32)
@@ -49,8 +49,8 @@
         toeplitz = jnp.concatenate(
             [jnp.where(upper, rolled[k + 1], rolled[k]) for k in range(sub_tiles)],
             axis=1).astype(jnp.bfloat16)
-        masked = jnp.where(lane_group == gg, w, jnp.zeros_like(w))
-        acc = acc + jnp.dot(toeplitz, masked, preferred_element_type=jnp.float32)
+        part = jnp.dot(toeplitz, w, preferred_element_type=jnp.float32)
+        acc = jnp.where(lane_group == gg, part, acc)
     conv = jnp.concatenate(
         [acc[:, i * LANES:(i + 1) * LANES] for i in range(out_tiles)], axis=0)
     cur = blocks[hops][...].astype(jnp.float32)

time: 99.6 us -> 97.4 us (0.978)
  Pallas kernels: 21.9 us -> 19.4 us
    pallas_call x1, Pallas kernels: 21.9 us -> 19.4 us  [convolve(): pl.pallas_call(kernel, grid=(chunks,), in_specs=[pl.BlockSpec((groups_per...]
where the time goes in v4:
time: 97.4 us; the launch traced here: 96.3 us
  waiting for transfers between devices  46.5 us (48%)
  blocking collectives  19.8 us (20%)
  Pallas kernels  19.4 us (20%)
  starting transfers between devices  3.84 us (4%)
  local copies, waits for them, and re-layouts  3.44 us (4%)
  other arithmetic  3.31 us (3%)
    ppermute x2, waiting for transfers between devices, from_behind(): return lax.ppermute(shard, axis, pairs)  44.2 us
    all_gather x1, blocking collectives, body(): all_taps = lax.all_gather(taps, 'seq', axis=0, tiled=True)  19.8 us
    pallas_call x1, Pallas kernels, convolve(): pl.pallas_call(kernel, grid=(chunks,), in_specs=[pl.BlockSpec((groups_per...  19.4 us
    ppermute x2, starting transfers between devices, from_behind(): return lax.ppermute(shard, axis, pairs)  3.83 us
    another operation x2, other arithmetic, body(): jnp.stack([jnp.where(first_core, signal, back_one), jnp.where(first_core,...  3.31 us
    ppermute x1, waiting for transfers between devices, body(): odd = lax.ppermute(outgoing, 'seq', swap)  2.26 us
  transfers between devices with their start and end apart: 3, of which 3 were waited for; matrix products, arithmetic and copies ran while one was open for 2% of the time, Pallas kernels for 0%

profile of v4, /device:TPU:8, one launch (start us, length us, event | category | flops | bytes accessed | tf_op | source)
XLA Modules:
  0.0 96.3 jit_solution(14823779004656905605)
XLA Ops:
  0.0 19.8 %all_gather.3 = bf16[1024,128]{1,0:T(8,128)(2,1)S(1)} all-gather(bf16[64,128]{1,0:T(8,128)(2,1)} %param.7), channel_id=1, replica_groups=mesh['rep'=2,'seq'=16] {'seq'}, dimensions={0}, use_global_device_ids=true | all-gather | bytes 278528 | tf_op jit(solution)/shard_map/all_gather | solution.py:93
  19.8 1.9 %collective-permute-start = (bf16[256,2048]{1,0:T(8,128)(2,1)}, bf16[256,2048]{1,0:T(8,128)(2,1)S(1)}, u32[]{:S(2)}, u32[]{:S(2)}) collective-permute-start(bf16[256,2048]{1,0:T(8,128)(2,1)} %refs_4_), channel_id=1, source_target_pairs={{0,4},{1,5},{2,6},{3,7},{4,8},{5,9},{6,10},{7,11},{8,12},{9,13},{1... | collective-permute-start | bytes 3145736 | tf_op jit(solution)/shard_map/ppermute | solution.py:17
  21.7 1.9 %collective-permute-start.1 = (bf16[256,2048]{1,0:T(8,128)(2,1)}, bf16[256,2048]{1,0:T(8,128)(2,1)S(1)}, u32[]{:S(2)}, u32[]{:S(2)}) collective-permute-start(bf16[256,2048]{1,0:T(8,128)(2,1)} %refs_4_), channel_id=1, source_target_pairs={{0,2},{1,3},{2,4},{3,5},{4,6},{5,7},{6,8},{7,9},{8,10},{9,11},{10,... | collective-permute-start | bytes 3145736 | tf_op jit(solution)/shard_map/ppermute | solution.py:17
  23.6 24.5 %collective-permute-done.refs_0_ = bf16[256,2048]{1,0:T(8,128)(2,1)S(1)} collective-permute-done((bf16[256,2048]{1,0:T(8,128)(2,1)}, bf16[256,2048]{1,0:T(8,128)(2,1)S(1)}, u32[]{:S(2)}, u32[]{:S(2)}) %collective-permute-start) | collective-permute-done | bytes 1048608 | tf_op jit(solution)/shard_map/ppermute | solution.py:17
  48.2 0.0 copy-start.1
  48.2 19.7 %collective-permute-done.1.refs_2_ = bf16[256,2048]{1,0:T(8,128)(2,1)S(1)} collective-permute-done((bf16[256,2048]{1,0:T(8,128)(2,1)}, bf16[256,2048]{1,0:T(8,128)(2,1)S(1)}, u32[]{:S(2)}, u32[]{:S(2)}) %collective-permute-start.1) | collective-permute-done | bytes 1048608 | tf_op jit(solution)/shard_map/ppermute | solution.py:17
  67.9 0.0 copy-start.2
  67.9 1.8 %select_bitcast_fusion.1 = (bf16[1,256,2048]{2,1,0:T(8,128)(2,1)S(1)}, bf16[1,256,2048]{2,1,0:T(8,128)(2,1)S(1)}) fusion(bf16[256,2048]{1,0:T(8,128)(2,1)} %refs_4_, bf16[256,2048]{1,0:T(8,128)(2,1)S(1)} %collective-permute-done.1.refs_2_, pred[]{:T(512)S(6)} %eq.5, bf16[256,2048]{1,0:T(8,128)(2,1)S(1)} %collective-permute-done.refs_0_), kind=kLoop, calls=%fused_computation.2 | loop fusion | flops 1048576 | bytes 5242881 | tf_op jit(solution)/shard_map/stack | solution.py:104
  69.6 0.0 copy-done.1
  69.7 0.0 copy-done.2
  69.7 1.5 %pad_maximum_fusion = bf16[2,256,2048]{2,1,0:T(8,128)(2,1)} fusion(bf16[1,256,2048]{2,1,0:T(8,128)(2,1)S(1)} %get-tuple-element.10, bf16[1,256,2048]{2,1,0:T(8,128)(2,1)S(1)} %get-tuple-element.9), kind=kLoop, calls=%fused_computation | loop fusion | flops 1048576 | bytes 4194304 | tf_op jit(solution)/shard_map/stack | solution.py:104
  71.2 0.0 collective-permute-start.2
  71.2 0.1 copy.6
  71.4 0.8 rev.3
  72.2 1.1 %concatenate.3.rows_ref = f32[128,1280]{1,0:T(8,128)} concatenate(f32[128,129]{1,0:T(8,128)S(1)} %broadcast_in_dim.6, bf16[128,1024]{1,0:T(8,128)(2,1)S(1)} %rev.3, f32[128,127]{1,0:T(8,128)S(1)} %broadcast_in_dim.7), dimensions={1} | concatenate | bytes 1048576 | tf_op jit(solution)/shard_map/concatenate | solution.py:25
  73.3 2.3 %collective-permute-done.2.refs_1_.refs_3_ = bf16[2,256,2048]{2,1,0:T(8,128)(2,1)S(1)} collective-permute-done((bf16[2,256,2048]{2,1,0:T(8,128)(2,1)}, bf16[2,256,2048]{2,1,0:T(8,128)(2,1)S(1)}, u32[]{:S(2)}, u32[]{:S(2)}) %collective-permute-start.2) | collective-permute-done | bytes 2097184 | tf_op jit(solution)/shard_map/ppermute | solution.py:108
  75.6 0.0 copy-start
  75.6 1.4 %copy-done = bf16[2,256,2048]{2,1,0:T(8,128)(2,1)} copy-done((bf16[2,256,2048]{2,1,0:T(8,128)(2,1)}, bf16[2,256,2048]{2,1,0:T(8,128)(2,1)S(1)}, u32[]{:S(2)}) %copy-start) | copy-done | bytes 2097176
  76.9 19.4 %shard_map.46 = bf16[256,2048]{1,0:T(8,128)(2,1)} custom-call(f32[128,1280]{1,0:T(8,128)} %concatenate.3.rows_ref, bf16[256,2048]{1,0:T(8,128)(2,1)} %copy-done.1, bf16[2,256,2048]{2,1,0:T(8,128)(2,1)} %copy-done, bf16[256,2048]{1,0:T(8,128)(2,1)} %copy-done.2, bf16[2,256,2048]{2,1,0:T(8,128)(2,1)} %copy-done, bf16[256,2048]{1,0:T(8,128)(2,1)} %refs_4_, ...), custom_call_target="tpu_custom_call" | custom-call | tf_op jit(solution)/shard_map/pallas_call | solution.py:77
  (2 shorter events, 0.0 us)
Async XLA Ops:
  19.8 28.4 %collective-permute-start = (bf16[256,2048]{1,0:T(8,128)(2,1)}, bf16[256,2048]{1,0:T(8,128)(2,1)S(1)}, u32[]{:S(2)}, u32[]{:S(2)}) collective-permute-start(bf16[256,2048]{1,0:T(8,128)(2,1)} %refs_4_), channel_id=1, source_target_pairs={{0,4},{1,5},{2,6},{3,7},{4,8},{5,9},{6,10},{7,11},{8,12},{9,13},{1... | collective-permute-start | bytes 3145736 | tf_op jit(solution)/shard_map/ppermute | solution.py:17
  21.7 46.2 %collective-permute-start.1 = (bf16[256,2048]{1,0:T(8,128)(2,1)}, bf16[256,2048]{1,0:T(8,128)(2,1)S(1)}, u32[]{:S(2)}, u32[]{:S(2)}) collective-permute-start(bf16[256,2048]{1,0:T(8,128)(2,1)} %refs_4_), channel_id=1, source_target_pairs={{0,2},{1,3},{2,4},{3,5},{4,6},{5,7},{6,8},{7,9},{8,10},{9,11},{10,... | collective-permute-start | bytes 3145736 | tf_op jit(solution)/shard_map/ppermute | solution.py:17
  48.2 21.5 %copy-start.1 = (bf16[256,2048]{1,0:T(8,128)(2,1)}, bf16[256,2048]{1,0:T(8,128)(2,1)S(1)}, u32[]{:S(2)}) copy-start(bf16[256,2048]{1,0:T(8,128)(2,1)S(1)} %collective-permute-done.refs_0_) | copy-start | bytes 3145732
  67.9 1.8 %copy-start.2 = (bf16[256,2048]{1,0:T(8,128)(2,1)}, bf16[256,2048]{1,0:T(8,128)(2,1)S(1)}, u32[]{:S(2)}) copy-start(bf16[256,2048]{1,0:T(8,128)(2,1)S(1)} %collective-permute-done.1.refs_2_) | copy-start | bytes 3145732
  71.2 4.4 %collective-permute-start.2 = (bf16[2,256,2048]{2,1,0:T(8,128)(2,1)}, bf16[2,256,2048]{2,1,0:T(8,128)(2,1)S(1)}, u32[]{:S(2)}, u32[]{:S(2)}) collective-permute-start(bf16[2,256,2048]{2,1,0:T(8,128)(2,1)} %pad_maximum_fusion), channel_id=1, source_target_pairs={{0,1},{1,0},{2,3},{3,2},{4,5},{5,4},{6,7},{7,6},{8,9},{9,8},{10,11... | collective-permute-start | bytes 6291464 | tf_op jit(solution)/shard_map/ppermute | solution.py:108
  75.6 1.4 %copy-start = (bf16[2,256,2048]{2,1,0:T(8,128)(2,1)}, bf16[2,256,2048]{2,1,0:T(8,128)(2,1)S(1)}, u32[]{:S(2)}) copy-start(bf16[2,256,2048]{2,1,0:T(8,128)(2,1)S(1)} %collective-permute-done.2.refs_1_.refs_3_) | copy-start | bytes 6291460

commit v5 on v4

v5 whole, which is shorter than its diff:
```python
import functools

import jax
import jax.numpy as jnp
from jax import lax
from jax.experimental import pallas as pl
from jax.experimental.pallas import tpu as pltpu
from jax.sharding import PartitionSpec as P

TILE = 128
LANES = 128


def from_behind(shard, axis, by):
    count = lax.axis_size(axis)
    pairs = [(i, i + by) for i in range(count) if 0 <= i + by < count]
    return lax.ppermute(shard, axis, pairs)


def tap_rows(all_taps, history):
    filter_len, group_count = all_taps.shape
    flipped = all_taps.T[:, ::-1].astype(jnp.float32)
    front = jnp.zeros((group_count, TILE + history - filter_len + 1), jnp.float32)
    back = jnp.zeros((group_count, TILE - 1), jnp.float32)
    return jnp.concatenate([front, flipped, back], axis=1)


def toeplitz(rows_ref, gg, k_lo, k_hi):
    upper = (lax.broadcasted_iota(jnp.int32, (TILE, TILE), 1)
             >= lax.broadcasted_iota(jnp.int32, (TILE, TILE), 0))
    rolled = {}
    for k in range(k_lo, k_hi + 2):
        window = jnp.broadcast_to(rows_ref[gg:gg + 1, k * TILE:(k + 1) * TILE], (TILE, TILE))
        rolled[k] = pltpu.roll(window, 0, 1, stride=1, stride_axis=0)
    return jnp.concatenate(
        [jnp.where(upper, rolled[k + 1], rolled[k]) for k in range(k_lo, k_hi + 1)],
        axis=1).astype(jnp.bfloat16)


def grouped_dot(rows_ref, w, k_lo, k_hi, group_width):
    lane_group = lax.broadcasted_iota(jnp.int32, (TILE, w.shape[1]), 1) % LANES // group_width
    acc = jnp.zeros((TILE, w.shape[1]), jnp.float32)
    for gg in range(rows_ref.shape[0]):
        part = jnp.dot(toeplitz(rows_ref, gg, k_lo, k_hi), w,
                       preferred_element_type=jnp.float32)
        acc = jnp.where(lane_group == gg, part, acc)
    return acc


def unfold(acc, out_tiles):
    return jnp.concatenate(
        [acc[:, i * LANES:(i + 1) * LANES] for i in range(out_tiles)], axis=0)


def own_kernel(rows_ref, cur_ref, out_ref, *, history_tiles, group_width):
    out_tiles = cur_ref.shape[0] // TILE
    k_lo = history_tiles - out_tiles + 1
    zero = jnp.zeros((TILE, LANES), cur_ref.dtype)
    columns = []
    for i in range(out_tiles):
        pieces = []
        for k in range(k_lo, history_tiles + 1):
            m = i + k - history_tiles
            pieces.append(cur_ref[m * TILE:(m + 1) * TILE, :] if m >= 0 else zero)
        columns.append(jnp.concatenate(pieces, axis=0))
    w = jnp.concatenate(columns, axis=1)
    acc = grouped_dot(rows_ref, w, k_lo, history_tiles, group_width)
    out_ref[...] = unfold(acc, out_tiles)


def history_kernel(rows_ref, *refs, hops, group_width):
    blocks = refs[:hops]
    own_ref, gate_ref, skip_ref, cur_ref, out_ref = refs[hops:]
    out_tiles = cur_ref.shape[0] // TILE
    x = jnp.concatenate([b[...] for b in blocks], axis=0)
    history_tiles = x.shape[0] // TILE
    zero = jnp.zeros((TILE, LANES), x.dtype)
    columns = [jnp.concatenate([x[i * TILE:]] + [zero] * i, axis=0) if i else x
               for i in range(out_tiles)]
    w = jnp.concatenate(columns, axis=1)
    acc = grouped_dot(rows_ref, w, 0, history_tiles - 1, group_width)
    conv = unfold(acc, out_tiles) + own_ref[...]
    cur = cur_ref[...].astype(jnp.float32)
    mixed = gate_ref[...].astype(jnp.float32) * (conv + skip_ref[...] * cur)
    out_ref[...] = mixed.astype(out_ref.dtype)


def own_terms(rows, signal, hops, group_width):
    block_rows, channels = signal.shape
    block_spec = pl.BlockSpec((block_rows, LANES), lambda c: (0, c))
    return pl.pallas_call(
        functools.partial(own_kernel, history_tiles=hops * block_rows // TILE,
                          group_width=group_width),
        grid=(channels // LANES,),
        in_specs=[pl.BlockSpec((LANES // group_width, rows.shape[1]), lambda c: (c, 0)),
                  block_spec],
        out_specs=block_spec,
        out_shape=jax.ShapeDtypeStruct(signal.shape, jnp.float32),
        compiler_params=pltpu.CompilerParams(dimension_semantics=("arbitrary",)),
    )(rows, signal)


def convolve(rows, blocks, own, gate, skip, signal, group_width):
    hops = len(blocks)
    block_rows, channels = gate.shape
    block_spec = pl.BlockSpec((block_rows, LANES), lambda c: (0, c))
    arrays, specs = [], []
    for block in blocks:
        if isinstance(block, tuple):
            arrays.append(block[0])
            specs.append(pl.BlockSpec((None, block_rows, LANES),
                                      lambda c, slot=block[1]: (slot, 0, c)))
        else:
            arrays.append(block)
            specs.append(block_spec)
    return pl.pallas_call(
        functools.partial(history_kernel, hops=hops, group_width=group_width),
        grid=(channels // LANES,),
        in_specs=[pl.BlockSpec((LANES // group_width, rows.shape[1]), lambda c: (c, 0))]
        + specs
        + [block_spec, block_spec, pl.BlockSpec((1, LANES), lambda c: (0, c)), block_spec],
        out_specs=block_spec,
        out_shape=jax.ShapeDtypeStruct(gate.shape, gate.dtype),
        compiler_params=pltpu.CompilerParams(dimension_semantics=("arbitrary",)),
    )(rows, *arrays, own, gate, skip.reshape(1, channels), signal)


def body(signal, gate, skip, taps):
    block_rows, channels = signal.shape
    group_count = taps.shape[1]
    group_width = channels // group_count
    all_taps = lax.all_gather(taps, "seq", axis=0, tiled=True)
    filter_len = all_taps.shape[0]
    hops = -(-(filter_len - 1) // block_rows)
    rows = tap_rows(all_taps, hops * block_rows)
    own = own_terms(rows, signal, hops, group_width)
    if hops != 4 or lax.axis_size("seq") % 2:
        received = [from_behind(signal, "seq", d) for d in range(hops, 0, -1)]
        return convolve(rows, received, own, gate, skip, signal, group_width)
    back_one = from_behind(signal, "seq", 2)
    back_two = from_behind(signal, "seq", 4)
    own, back_one, back_two = lax.optimization_barrier((own, back_one, back_two))
    first_core = lax.axis_index("seq") % 2 == 0
    outgoing = jnp.stack([jnp.where(first_core, signal, back_one),
                          jnp.where(first_core, back_one, back_two)])
    count = lax.axis_size("seq")
    swap = [(i, i ^ 1) for i in range(count)]
    odd = lax.ppermute(outgoing, "seq", swap)
    return convolve(rows, [back_two, (odd, 1), back_one, (odd, 0)], own,
                    gate, skip, signal, group_width)


def solution(mesh):
    placed = (P(("rep", "seq"), None), P(("rep", "seq"), None), P(), P("seq", None))
    return jax.shard_map(
        body, mesh=mesh, in_specs=placed, out_specs=P(("rep", "seq"), None), check_vma=False
    )
```

time: 97.4 us -> 104 us (1.068)
  the two profiles are of different devices: /device:TPU:8 before, /device:TPU:5 now
where the time goes in v5:
time: 104 us; the launch traced here: 103 us
  blocking collectives  56.7 us (55%)
  Pallas kernels  30.4 us (29%)
  starting transfers between devices  6.58 us (6%)
  local copies, waits for them, and re-layouts  4.56 us (4%)
  waiting for transfers between devices  4 us (4%)
    all_gather x1, blocking collectives, body(): all_taps = lax.all_gather(taps, 'seq', axis=0, tiled=True)  56.7 us
    pallas_call x1, Pallas kernels, convolve(): pl.pallas_call(functools.partial(history_kernel, hops=hops, group_width=g...  18.4 us
    pallas_call x1, Pallas kernels, own_terms(): pl.pallas_call(functools.partial(own_kernel, history_tiles=hops * block_r...  12 us
    ppermute x2, starting transfers between devices, from_behind(): return lax.ppermute(shard, axis, pairs)  6.34 us
    ppermute x1, waiting for transfers between devices, body(): odd = lax.ppermute(outgoing, 'seq', swap)  3.99 us
    unnamed x8, local copies, waits for them, and re-layouts  2.47 us
  transfers between devices with their start and end apart: 3, of which 1 were waited for; matrix products, arithmetic and copies ran while one was open for 2% of the time, Pallas kernels for 12%

profile of v5, /device:TPU:5, one launch (start us, length us, event | category | flops | bytes accessed | tf_op | source)
XLA Modules:
  0.0 102.7 jit_solution(9428164765028733048)
XLA Ops:
  0.0 3.3 %collective-permute-start.1 = (bf16[256,2048]{1,0:T(8,128)(2,1)}, bf16[256,2048]{1,0:T(8,128)(2,1)S(1)}, u32[]{:S(2)}, u32[]{:S(2)}) collective-permute-start(bf16[256,2048]{1,0:T(8,128)(2,1)} %refs_7_.1), channel_id=1, source_target_pairs={{0,4},{1,5},{2,6},{3,7},{4,8},{5,9},{6,10},{7,11},{8,12},{9,13},{1... | collective-permute-start | bytes 3145736 | tf_op jit(solution)/shard_map/ppermute | solution.py:17
  3.3 3.1 %collective-permute-start = (bf16[256,2048]{1,0:T(8,128)(2,1)}, bf16[256,2048]{1,0:T(8,128)(2,1)S(1)}, u32[]{:S(2)}, u32[]{:S(2)}) collective-permute-start(bf16[256,2048]{1,0:T(8,128)(2,1)} %refs_7_.1), channel_id=1, source_target_pairs={{0,2},{1,3},{2,4},{3,5},{4,6},{5,7},{6,8},{7,9},{8,10},{9,11},{10,... | collective-permute-start | bytes 3145736 | tf_op jit(solution)/shard_map/ppermute | solution.py:17
  6.4 56.7 %all_gather.3 = bf16[1024,128]{1,0:T(8,128)(2,1)S(1)} all-gather(bf16[64,128]{1,0:T(8,128)(2,1)} %param.7), channel_id=1, replica_groups=mesh['rep'=2,'seq'=16] {'seq'}, dimensions={0}, use_global_device_ids=true | all-gather | bytes 278528 | tf_op jit(solution)/shard_map/all_gather | solution.py:132
  63.1 0.1 copy.6
  63.3 0.8 rev.3
  64.2 1.1 %concatenate.3.rows_ref = f32[128,1280]{1,0:T(8,128)} concatenate(f32[128,129]{1,0:T(8,128)S(1)} %broadcast_in_dim.6, bf16[128,1024]{1,0:T(8,128)(2,1)S(1)} %rev.3, f32[128,127]{1,0:T(8,128)S(1)} %broadcast_in_dim.7), dimensions={1} | concatenate | bytes 1048576 | tf_op jit(solution)/shard_map/concatenate | solution.py:25
  65.2 0.0 copy-start
  65.2 12.0 %shard_map.46.refs_4_ = f32[256,2048]{1,0:T(8,128)} custom-call(f32[128,1280]{1,0:T(8,128)} %concatenate.3.rows_ref, bf16[256,2048]{1,0:T(8,128)(2,1)} %refs_7_.1), custom_call_target="tpu_custom_call" | custom-call | tf_op jit(solution)/shard_map/pallas_call | solution.py:91
  77.2 0.0 collective-permute-done.1.refs_0_
  77.2 0.0 copy-start.2
  77.2 0.0 collective-permute-done.refs_2_
  77.2 0.0 copy-done
  77.2 0.0 copy-start.3
  77.3 0.2 select_bitcast_fusion.1
  77.4 0.8 copy-done.2
  78.2 0.4 copy-done.3
  78.6 0.2 pad_maximum_fusion
  78.8 0.2 collective-permute-start.2
  79.0 4.0 %collective-permute-done.2.refs_1_.refs_3_ = bf16[2,256,2048]{2,1,0:T(8,128)(2,1)S(1)} collective-permute-done((bf16[2,256,2048]{2,1,0:T(8,128)(2,1)S(1)}, bf16[2,256,2048]{2,1,0:T(8,128)(2,1)S(1)}, u32[]{:S(2)}, u32[]{:S(2)}) %collective-permute-start.2) | collective-permute-done | bytes 2097184 | tf_op jit(solution)/shard_map/ppermute | solution.py:148
  83.0 0.0 copy-start.1
  83.0 1.3 %copy-done.1 = bf16[2,256,2048]{2,1,0:T(8,128)(2,1)} copy-done((bf16[2,256,2048]{2,1,0:T(8,128)(2,1)}, bf16[2,256,2048]{2,1,0:T(8,128)(2,1)S(1)}, u32[]{:S(2)}) %copy-start.1) | copy-done | bytes 2097176
  84.3 18.4 %shard_map.47 = bf16[256,2048]{1,0:T(8,128)(2,1)} custom-call(f32[128,1280]{1,0:T(8,128)} %concatenate.3.rows_ref, bf16[256,2048]{1,0:T(8,128)(2,1)} %copy-done.2, bf16[2,256,2048]{2,1,0:T(8,128)(2,1)} %copy-done.1, bf16[256,2048]{1,0:T(8,128)(2,1)} %copy-done.3, bf16[2,256,2048]{2,1,0:T(8,128)(2,1)} %copy-done.1, f32[256,2048]{1,0:T(8,128)} %shard_map.46.refs_4_, ...), custom_call_target="tpu_custom_call" | custom-call | tf_op jit(solution)/shard_map/pallas_call | solution.py:116
  (2 shorter events, 0.0 us)
Async XLA Ops:
  0.0 77.2 %collective-permute-start.1 = (bf16[256,2048]{1,0:T(8,128)(2,1)}, bf16[256,2048]{1,0:T(8,128)(2,1)S(1)}, u32[]{:S(2)}, u32[]{:S(2)}) collective-permute-start(bf16[256,2048]{1,0:T(8,128)(2,1)} %refs_7_.1), channel_id=1, source_target_pairs={{0,4},{1,5},{2,6},{3,7},{4,8},{5,9},{6,10},{7,11},{8,12},{9,13},{1... | collective-permute-start | bytes 3145736 | tf_op jit(solution)/shard_map/ppermute | solution.py:17
  3.3 74.0 %collective-permute-start = (bf16[256,2048]{1,0:T(8,128)(2,1)}, bf16[256,2048]{1,0:T(8,128)(2,1)S(1)}, u32[]{:S(2)}, u32[]{:S(2)}) collective-permute-start(bf16[256,2048]{1,0:T(8,128)(2,1)} %refs_7_.1), channel_id=1, source_target_pairs={{0,2},{1,3},{2,4},{3,5},{4,6},{5,7},{6,8},{7,9},{8,10},{9,11},{10,... | collective-permute-start | bytes 3145736 | tf_op jit(solution)/shard_map/ppermute | solution.py:17
  65.2 12.0 %copy-start = (bf16[256,2048]{1,0:T(8,128)(2,1)S(1)}, bf16[256,2048]{1,0:T(8,128)(2,1)}, u32[]{:S(2)}) copy-start(bf16[256,2048]{1,0:T(8,128)(2,1)} %refs_7_.1) | copy-start | bytes 3145732
  77.2 1.0 copy-start.2
  77.2 1.3 %copy-start.3 = (bf16[256,2048]{1,0:T(8,128)(2,1)}, bf16[256,2048]{1,0:T(8,128)(2,1)S(1)}, u32[]{:S(2)}) copy-start(bf16[256,2048]{1,0:T(8,128)(2,1)S(1)} %collective-permute-done.refs_2_) | copy-start | bytes 3145732
  78.8 4.2 %collective-permute-start.2 = (bf16[2,256,2048]{2,1,0:T(8,128)(2,1)S(1)}, bf16[2,256,2048]{2,1,0:T(8,128)(2,1)S(1)}, u32[]{:S(2)}, u32[]{:S(2)}) collective-permute-start(bf16[2,256,2048]{2,1,0:T(8,128)(2,1)S(1)} %pad_maximum_fusion), channel_id=1, source_target_pairs={{0,1},{1,0},{2,3},{3,2},{4,5},{5,4},{6,7},{7,6},{8,9},{9,8},{10,11... | collective-permute-start | bytes 6291464 | tf_op jit(solution)/shard_map/ppermute | solution.py:148
  83.0 1.3 %copy-start.1 = (bf16[2,256,2048]{2,1,0:T(8,128)(2,1)}, bf16[2,256,2048]{2,1,0:T(8,128)(2,1)S(1)}, u32[]{:S(2)}) copy-start(bf16[2,256,2048]{2,1,0:T(8,128)(2,1)S(1)} %collective-permute-done.2.refs_1_.refs_3_) | copy-start | bytes 6291460

commit v6 on v4

--- a/solution.py
+++ b/solution.py
@@ -39,18 +39,20 @@
     lane_group = lax.broadcasted_iota(jnp.int32, (TILE, w.shape[1]), 1) % LANES // group_width
     upper = (lax.broadcasted_iota(jnp.int32, (TILE, TILE), 1)
              >= lax.broadcasted_iota(jnp.int32, (TILE, TILE), 0))
-    acc = jnp.zeros((TILE, w.shape[1]), jnp.float32)
+    toeplitz = []
     for gg in range(groups_here):
         rolled = []
         for k in range(sub_tiles + 1):
             window = rows_ref[gg:gg + 1, k * TILE:(k + 1) * TILE]
             window = jnp.broadcast_to(window, (TILE, TILE))
             rolled.append(pltpu.roll(window, 0, 1, stride=1, stride_axis=0))
-        toeplitz = jnp.concatenate(
+        toeplitz.append(jnp.concatenate(
             [jnp.where(upper, rolled[k + 1], rolled[k]) for k in range(sub_tiles)],
-            axis=1).astype(jnp.bfloat16)
-        part = jnp.dot(toeplitz, w, preferred_element_type=jnp.float32)
-        acc = jnp.where(lane_group == gg, part, acc)
+            axis=1).astype(jnp.bfloat16))
+    part = jnp.dot(jnp.concatenate(toeplitz, axis=0), w, preferred_element_type=jnp.float32)
+    acc = part[0:TILE]
+    for gg in range(1, groups_here):
+        acc = jnp.where(lane_group == gg, part[gg * TILE:(gg + 1) * TILE], acc)
     conv = jnp.concatenate(
         [acc[:, i * LANES:(i + 1) * LANES] for i in range(out_tiles)], axis=0)
     cur = blocks[hops][...].astype(jnp.float32)

time: 97.4 us -> 97.6 us (level)
  no operation moved by 1% of the time
where the time goes in v6:
time: 97.6 us; the launch traced here: 96.8 us
  waiting for transfers between devices  46.5 us (48%)
  Pallas kernels  19.9 us (20%)
  blocking collectives  19.8 us (20%)
  starting transfers between devices  3.84 us (4%)
  local copies, waits for them, and re-layouts  3.44 us (4%)
  other arithmetic  3.31 us (3%)
    ppermute x2, waiting for transfers between devices, from_behind(): return lax.ppermute(shard, axis, pairs)  44.2 us
    pallas_call x1, Pallas kernels, convolve(): pl.pallas_call(kernel, grid=(chunks,), in_specs=[pl.BlockSpec((groups_per...  19.9 us
    all_gather x1, blocking collectives, body(): all_taps = lax.all_gather(taps, 'seq', axis=0, tiled=True)  19.8 us
    ppermute x2, starting transfers between devices, from_behind(): return lax.ppermute(shard, axis, pairs)  3.83 us
    another operation x2, other arithmetic, body(): jnp.stack([jnp.where(first_core, signal, back_one), jnp.where(first_core,...  3.31 us
    ppermute x1, waiting for transfers between devices, body(): odd = lax.ppermute(outgoing, 'seq', swap)  2.26 us
  transfers between devices with their start and end apart: 3, of which 3 were waited for; matrix products, arithmetic and copies ran while one was open for 2% of the time, Pallas kernels for 0%

profile of v6, /device:TPU:8, one launch (start us, length us, event | category | flops | bytes accessed | tf_op | source)
XLA Modules:
  0.0 96.8 jit_solution(17993895994356286051)
XLA Ops:
  0.0 19.8 %all_gather.3 = bf16[1024,128]{1,0:T(8,128)(2,1)S(1)} all-gather(bf16[64,128]{1,0:T(8,128)(2,1)} %param.7), channel_id=1, replica_groups=mesh['rep'=2,'seq'=16] {'seq'}, dimensions={0}, use_global_device_ids=true | all-gather | bytes 278528 | tf_op jit(solution)/shard_map/all_gather | solution.py:95
  19.8 1.9 %collective-permute-start = (bf16[256,2048]{1,0:T(8,128)(2,1)}, bf16[256,2048]{1,0:T(8,128)(2,1)S(1)}, u32[]{:S(2)}, u32[]{:S(2)}) collective-permute-start(bf16[256,2048]{1,0:T(8,128)(2,1)} %refs_4_), channel_id=1, source_target_pairs={{0,4},{1,5},{2,6},{3,7},{4,8},{5,9},{6,10},{7,11},{8,12},{9,13},{1... | collective-permute-start | bytes 3145736 | tf_op jit(solution)/shard_map/ppermute | solution.py:17
  21.7 1.9 %collective-permute-start.1 = (bf16[256,2048]{1,0:T(8,128)(2,1)}, bf16[256,2048]{1,0:T(8,128)(2,1)S(1)}, u32[]{:S(2)}, u32[]{:S(2)}) collective-permute-start(bf16[256,2048]{1,0:T(8,128)(2,1)} %refs_4_), channel_id=1, source_target_pairs={{0,2},{1,3},{2,4},{3,5},{4,6},{5,7},{6,8},{7,9},{8,10},{9,11},{10,... | collective-permute-start | bytes 3145736 | tf_op jit(solution)/shard_map/ppermute | solution.py:17
  23.6 24.5 %collective-permute-done.refs_0_ = bf16[256,2048]{1,0:T(8,128)(2,1)S(1)} collective-permute-done((bf16[256,2048]{1,0:T(8,128)(2,1)}, bf16[256,2048]{1,0:T(8,128)(2,1)S(1)}, u32[]{:S(2)}, u32[]{:S(2)}) %collective-permute-start) | collective-permute-done | bytes 1048608 | tf_op jit(solution)/shard_map/ppermute | solution.py:17
  48.2 0.0 copy-start.1
  48.2 19.7 %collective-permute-done.1.refs_2_ = bf16[256,2048]{1,0:T(8,128)(2,1)S(1)} collective-permute-done((bf16[256,2048]{1,0:T(8,128)(2,1)}, bf16[256,2048]{1,0:T(8,128)(2,1)S(1)}, u32[]{:S(2)}, u32[]{:S(2)}) %collective-permute-start.1) | collective-permute-done | bytes 1048608 | tf_op jit(solution)/shard_map/ppermute | solution.py:17
  67.9 0.0 copy-start.2
  67.9 1.8 %select_bitcast_fusion.1 = (bf16[1,256,2048]{2,1,0:T(8,128)(2,1)S(1)}, bf16[1,256,2048]{2,1,0:T(8,128)(2,1)S(1)}) fusion(bf16[256,2048]{1,0:T(8,128)(2,1)} %refs_4_, bf16[256,2048]{1,0:T(8,128)(2,1)S(1)} %collective-permute-done.1.refs_2_, pred[]{:T(512)S(6)} %eq.5, bf16[256,2048]{1,0:T(8,128)(2,1)S(1)} %collective-permute-done.refs_0_), kind=kLoop, calls=%fused_computation.2 | loop fusion | flops 1048576 | bytes 5242881 | tf_op jit(solution)/shard_map/stack | solution.py:106
  69.6 0.0 copy-done.1
  69.7 0.0 copy-done.2
  69.7 1.5 %pad_maximum_fusion = bf16[2,256,2048]{2,1,0:T(8,128)(2,1)} fusion(bf16[1,256,2048]{2,1,0:T(8,128)(2,1)S(1)} %get-tuple-element.10, bf16[1,256,2048]{2,1,0:T(8,128)(2,1)S(1)} %get-tuple-element.9), kind=kLoop, calls=%fused_computation | loop fusion | flops 1048576 | bytes 4194304 | tf_op jit(solution)/shard_map/stack | solution.py:106
  71.2 0.0 collective-permute-start.2
  71.2 0.1 copy.6
  71.4 0.8 rev.3
  72.2 1.1 %concatenate.3.rows_ref = f32[128,1280]{1,0:T(8,128)} concatenate(f32[128,129]{1,0:T(8,128)S(1)} %broadcast_in_dim.6, bf16[128,1024]{1,0:T(8,128)(2,1)S(1)} %rev.3, f32[128,127]{1,0:T(8,128)S(1)} %broadcast_in_dim.7), dimensions={1} | concatenate | bytes 1048576 | tf_op jit(solution)/shard_map/concatenate | solution.py:25
  73.3 2.3 %collective-permute-done.2.refs_1_.refs_3_ = bf16[2,256,2048]{2,1,0:T(8,128)(2,1)S(1)} collective-permute-done((bf16[2,256,2048]{2,1,0:T(8,128)(2,1)}, bf16[2,256,2048]{2,1,0:T(8,128)(2,1)S(1)}, u32[]{:S(2)}, u32[]{:S(2)}) %collective-permute-start.2) | collective-permute-done | bytes 2097184 | tf_op jit(solution)/shard_map/ppermute | solution.py:110
  75.6 0.0 copy-start
  75.6 1.4 %copy-done = bf16[2,256,2048]{2,1,0:T(8,128)(2,1)} copy-done((bf16[2,256,2048]{2,1,0:T(8,128)(2,1)}, bf16[2,256,2048]{2,1,0:T(8,128)(2,1)S(1)}, u32[]{:S(2)}) %copy-start) | copy-done | bytes 2097176
  76.9 19.9 %shard_map.46 = bf16[256,2048]{1,0:T(8,128)(2,1)} custom-call(f32[128,1280]{1,0:T(8,128)} %concatenate.3.rows_ref, bf16[256,2048]{1,0:T(8,128)(2,1)} %copy-done.1, bf16[2,256,2048]{2,1,0:T(8,128)(2,1)} %copy-done, bf16[256,2048]{1,0:T(8,128)(2,1)} %copy-done.2, bf16[2,256,2048]{2,1,0:T(8,128)(2,1)} %copy-done, bf16[256,2048]{1,0:T(8,128)(2,1)} %refs_4_, ...), custom_call_target="tpu_custom_call" | custom-call | tf_op jit(solution)/shard_map/pallas_call | solution.py:79
  (2 shorter events, 0.0 us)
Async XLA Ops:
  19.8 28.4 %collective-permute-start = (bf16[256,2048]{1,0:T(8,128)(2,1)}, bf16[256,2048]{1,0:T(8,128)(2,1)S(1)}, u32[]{:S(2)}, u32[]{:S(2)}) collective-permute-start(bf16[256,2048]{1,0:T(8,128)(2,1)} %refs_4_), channel_id=1, source_target_pairs={{0,4},{1,5},{2,6},{3,7},{4,8},{5,9},{6,10},{7,11},{8,12},{9,13},{1... | collective-permute-start | bytes 3145736 | tf_op jit(solution)/shard_map/ppermute | solution.py:17
  21.7 46.2 %collective-permute-start.1 = (bf16[256,2048]{1,0:T(8,128)(2,1)}, bf16[256,2048]{1,0:T(8,128)(2,1)S(1)}, u32[]{:S(2)}, u32[]{:S(2)}) collective-permute-start(bf16[256,2048]{1,0:T(8,128)(2,1)} %refs_4_), channel_id=1, source_target_pairs={{0,2},{1,3},{2,4},{3,5},{4,6},{5,7},{6,8},{7,9},{8,10},{9,11},{10,... | collective-permute-start | bytes 3145736 | tf_op jit(solution)/shard_map/ppermute | solution.py:17
  48.2 21.5 %copy-start.1 = (bf16[256,2048]{1,0:T(8,128)(2,1)}, bf16[256,2048]{1,0:T(8,128)(2,1)S(1)}, u32[]{:S(2)}) copy-start(bf16[256,2048]{1,0:T(8,128)(2,1)S(1)} %collective-permute-done.refs_0_) | copy-start | bytes 3145732
  67.9 1.8 %copy-start.2 = (bf16[256,2048]{1,0:T(8,128)(2,1)}, bf16[256,2048]{1,0:T(8,128)(2,1)S(1)}, u32[]{:S(2)}) copy-start(bf16[256,2048]{1,0:T(8,128)(2,1)S(1)} %collective-permute-done.1.refs_2_) | copy-start | bytes 3145732
  71.2 4.4 %collective-permute-start.2 = (bf16[2,256,2048]{2,1,0:T(8,128)(2,1)}, bf16[2,256,2048]{2,1,0:T(8,128)(2,1)S(1)}, u32[]{:S(2)}, u32[]{:S(2)}) collective-permute-start(bf16[2,256,2048]{2,1,0:T(8,128)(2,1)} %pad_maximum_fusion), channel_id=1, source_target_pairs={{0,1},{1,0},{2,3},{3,2},{4,5},{5,4},{6,7},{7,6},{8,9},{9,8},{10,11... | collective-permute-start | bytes 6291464 | tf_op jit(solution)/shard_map/ppermute | solution.py:110
  75.6 1.4 %copy-start = (bf16[2,256,2048]{2,1,0:T(8,128)(2,1)}, bf16[2,256,2048]{2,1,0:T(8,128)(2,1)S(1)}, u32[]{:S(2)}) copy-start(bf16[2,256,2048]{2,1,0:T(8,128)(2,1)S(1)} %collective-permute-done.2.refs_1_.refs_3_) | copy-start | bytes 6291460

commit v7 on v4

--- a/solution.py
+++ b/solution.py
@@ -90,7 +90,9 @@
     block_rows, channels = signal.shape
     group_count = taps.shape[1]
     group_width = channels // group_count
-    all_taps = lax.all_gather(taps, "seq", axis=0, tiled=True)
+    count = lax.axis_size("seq")
+    spread = jnp.concatenate([taps] * count, axis=0)
+    all_taps = lax.all_to_all(spread, "seq", 0, 0, tiled=True)
     filter_len = all_taps.shape[0]
     hops = -(-(filter_len - 1) // block_rows)
     all_taps, signal = lax.optimization_barrier((all_taps, signal))
@@ -103,7 +105,6 @@
     first_core = lax.axis_index("seq") % 2 == 0
     outgoing = jnp.stack([jnp.where(first_core, signal, back_one),
                           jnp.where(first_core, back_one, back_two)])
-    count = lax.axis_size("seq")
     swap = [(i, i ^ 1) for i in range(count)]
     odd = lax.ppermute(outgoing, "seq", swap)
     return convolve(rows, [back_two, (odd, 1), back_one, (odd, 0), signal],

time: 97.4 us -> 107 us (1.099); the launches traced: 96.3 us -> 105 us
  local copies, waits for them, and re-layouts: 3.44 us -> 15 us
  blocking collectives: 19.8 us -> 13.6 us
  starting transfers between devices: 3.84 us -> 5.96 us
    all_gather x1 -> x0, blocking collectives: 19.8 us -> none  [body(): all_taps = lax.all_gather(taps, 'seq', axis=0, tiled=True)]
    all_to_all x0 -> x1, blocking collectives: none -> 13.6 us  [body(): all_taps = lax.all_to_all(spread, 'seq', 0, 0, tiled=True)]
    unnamed x6 -> x21, local copies, waits for them, and re-layouts: 1.36 us -> 12.2 us
    ppermute x2, starting transfers between devices: 3.83 us -> 5.96 us  [from_behind(): return lax.ppermute(shard, axis, pairs)]
where the time goes in v7:
time: 107 us; the launch traced here: 105 us
  waiting for transfers between devices  47.3 us (44%)
  Pallas kernels  19.4 us (18%)
  local copies, waits for them, and re-layouts  15 us (14%)
  blocking collectives  13.6 us (13%)
  starting transfers between devices  5.96 us (6%)
  other arithmetic  3.31 us (3%)
    ppermute x2, waiting for transfers between devices, from_behind(): return lax.ppermute(shard, axis, pairs)  45 us
    pallas_call x1, Pallas kernels, convolve(): pl.pallas_call(kernel, grid=(chunks,), in_specs=[pl.BlockSpec((groups_per...  19.4 us
    all_to_all x1, blocking collectives, body(): all_taps = lax.all_to_all(spread, 'seq', 0, 0, tiled=True)  13.6 us
    unnamed x21, local copies, waits for them, and re-layouts  12.2 us
    ppermute x2, starting transfers between devices, from_behind(): return lax.ppermute(shard, axis, pairs)  5.96 us
    another operation x2, other arithmetic, body(): jnp.stack([jnp.where(first_core, signal, back_one), jnp.where(first_core,...  3.31 us
    ppermute x1, waiting for transfers between devices, body(): odd = lax.ppermute(outgoing, 'seq', swap)  2.26 us
  transfers between devices with their start and end apart: 3, of which 3 were waited for; matrix products, arithmetic and copies ran while one was open for 2% of the time, Pallas kernels for 0%

profile of v7, /device:TPU:8, one launch (start us, length us, event | category | flops | bytes accessed | tf_op | source)
XLA Modules:
  0.0 104.7 jit_solution(12657899251327918374)
XLA Ops:
  0.0 0.7 constant_dynamic-update-slice_fusion.15
  0.7 0.7 constant_dynamic-update-slice_fusion.14
  1.4 0.7 constant_dynamic-update-slice_fusion.13
  2.2 0.7 constant_dynamic-update-slice_fusion.12
  2.9 0.7 constant_dynamic-update-slice_fusion.11
  3.6 0.7 constant_dynamic-update-slice_fusion.10
  4.3 0.7 constant_dynamic-update-slice_fusion.9
  5.1 0.7 constant_dynamic-update-slice_fusion.8
  5.8 0.7 constant_dynamic-update-slice_fusion.7
  6.5 0.7 constant_dynamic-update-slice_fusion.6
  7.2 0.7 constant_dynamic-update-slice_fusion.5
  8.0 0.7 constant_dynamic-update-slice_fusion.4
  8.7 0.7 constant_dynamic-update-slice_fusion.3
  9.4 0.7 constant_dynamic-update-slice_fusion.2
  10.1 0.7 constant_dynamic-update-slice_fusion.1
  10.9 0.7 constant_dynamic-update-slice_fusion
  11.6 13.6 %all_to_all.12 = bf16[16,64,128]{2,1,0:T(8,128)(2,1)S(1)} all-to-all(bf16[16,64,128]{2,1,0:T(8,128)(2,1)S(1)} %bitcast.10), channel_id=1, replica_groups=mesh['rep'=2,'seq'=16] {'seq'}, dimensions={0} | all-to-all | bytes 524288 | tf_op jit(solution)/shard_map/all_to_all | solution.py:95
  25.2 4.0 %collective-permute-start = (bf16[256,2048]{1,0:T(8,128)(2,1)}, bf16[256,2048]{1,0:T(8,128)(2,1)S(1)}, u32[]{:S(2)}, u32[]{:S(2)}) collective-permute-start(bf16[256,2048]{1,0:T(8,128)(2,1)} %refs_4_), channel_id=1, source_target_pairs={{0,4},{1,5},{2,6},{3,7},{4,8},{5,9},{6,10},{7,11},{8,12},{9,13},{1... | collective-permute-start | bytes 3145736 | tf_op jit(solution)/shard_map/ppermute | solution.py:17
  29.3 1.9 %collective-permute-start.1 = (bf16[256,2048]{1,0:T(8,128)(2,1)}, bf16[256,2048]{1,0:T(8,128)(2,1)S(1)}, u32[]{:S(2)}, u32[]{:S(2)}) collective-permute-start(bf16[256,2048]{1,0:T(8,128)(2,1)} %refs_4_), channel_id=1, source_target_pairs={{0,2},{1,3},{2,4},{3,5},{4,6},{5,7},{6,8},{7,9},{8,10},{9,11},{10,... | collective-permute-start | bytes 3145736 | tf_op jit(solution)/shard_map/ppermute | solution.py:17
  31.2 21.9 %collective-permute-done.refs_0_ = bf16[256,2048]{1,0:T(8,128)(2,1)S(1)} collective-permute-done((bf16[256,2048]{1,0:T(8,128)(2,1)}, bf16[256,2048]{1,0:T(8,128)(2,1)S(1)}, u32[]{:S(2)}, u32[]{:S(2)}) %collective-permute-start) | collective-permute-done | bytes 1048608 | tf_op jit(solution)/shard_map/ppermute | solution.py:17
  53.1 0.0 copy-start.1
  53.1 23.2 %collective-permute-done.1.refs_2_ = bf16[256,2048]{1,0:T(8,128)(2,1)S(1)} collective-permute-done((bf16[256,2048]{1,0:T(8,128)(2,1)}, bf16[256,2048]{1,0:T(8,128)(2,1)S(1)}, u32[]{:S(2)}, u32[]{:S(2)}) %collective-permute-start.1) | collective-permute-done | bytes 1048608 | tf_op jit(solution)/shard_map/ppermute | solution.py:17
  76.3 0.0 copy-start.2
  76.3 1.8 %select_bitcast_fusion.1 = (bf16[1,256,2048]{2,1,0:T(8,128)(2,1)S(1)}, bf16[1,256,2048]{2,1,0:T(8,128)(2,1)S(1)}) fusion(bf16[256,2048]{1,0:T(8,128)(2,1)} %refs_4_, bf16[256,2048]{1,0:T(8,128)(2,1)S(1)} %collective-permute-done.1.refs_2_, pred[]{:T(512)S(6)} %eq.5, bf16[256,2048]{1,0:T(8,128)(2,1)S(1)} %collective-permute-done.refs_0_), kind=kLoop, calls=%fused_computation.2 | loop fusion | flops 1048576 | bytes 5242881 | tf_op jit(solution)/shard_map/stack | solution.py:106
  78.0 0.0 copy-done.1
  78.1 0.0 copy-done.2
  78.1 1.5 %pad_maximum_fusion = bf16[2,256,2048]{2,1,0:T(8,128)(2,1)} fusion(bf16[1,256,2048]{2,1,0:T(8,128)(2,1)S(1)} %get-tuple-element.10, bf16[1,256,2048]{2,1,0:T(8,128)(2,1)S(1)} %get-tuple-element.9), kind=kLoop, calls=%fused_computation | loop fusion | flops 1048576 | bytes 4194304 | tf_op jit(solution)/shard_map/stack | solution.py:106
  79.6 0.0 collective-permute-start.2
  79.6 0.1 copy.6
  79.8 0.8 rev.3
  80.6 1.1 %concatenate.7.rows_ref = f32[128,1280]{1,0:T(8,128)} concatenate(f32[128,129]{1,0:T(8,128)S(1)} %broadcast_in_dim.6, bf16[128,1024]{1,0:T(8,128)(2,1)S(1)} %rev.3, f32[128,127]{1,0:T(8,128)S(1)} %broadcast_in_dim.7), dimensions={1} | concatenate | bytes 1048576 | tf_op jit(solution)/shard_map/concatenate | solution.py:25
  81.7 2.3 %collective-permute-done.2.refs_1_.refs_3_ = bf16[2,256,2048]{2,1,0:T(8,128)(2,1)S(1)} collective-permute-done((bf16[2,256,2048]{2,1,0:T(8,128)(2,1)}, bf16[2,256,2048]{2,1,0:T(8,128)(2,1)S(1)}, u32[]{:S(2)}, u32[]{:S(2)}) %collective-permute-start.2) | collective-permute-done | bytes 2097184 | tf_op jit(solution)/shard_map/ppermute | solution.py:109
  84.0 0.0 copy-start
  84.0 1.4 %copy-done = bf16[2,256,2048]{2,1,0:T(8,128)(2,1)} copy-done((bf16[2,256,2048]{2,1,0:T(8,128)(2,1)}, bf16[2,256,2048]{2,1,0:T(8,128)(2,1)S(1)}, u32[]{:S(2)}) %copy-start) | copy-done | bytes 2097176
  85.3 19.4 %shard_map.46 = bf16[256,2048]{1,0:T(8,128)(2,1)} custom-call(f32[128,1280]{1,0:T(8,128)} %concatenate.7.rows_ref, bf16[256,2048]{1,0:T(8,128)(2,1)} %copy-done.1, bf16[2,256,2048]{2,1,0:T(8,128)(2,1)} %copy-done, bf16[256,2048]{1,0:T(8,128)(2,1)} %copy-done.2, bf16[2,256,2048]{2,1,0:T(8,128)(2,1)} %copy-done, bf16[256,2048]{1,0:T(8,128)(2,1)} %refs_4_, ...), custom_call_target="tpu_custom_call" | custom-call | tf_op jit(solution)/shard_map/pallas_call | solution.py:77
  (2 shorter events, 0.0 us)
Async XLA Ops:
  25.2 27.9 %collective-permute-start = (bf16[256,2048]{1,0:T(8,128)(2,1)}, bf16[256,2048]{1,0:T(8,128)(2,1)S(1)}, u32[]{:S(2)}, u32[]{:S(2)}) collective-permute-start(bf16[256,2048]{1,0:T(8,128)(2,1)} %refs_4_), channel_id=1, source_target_pairs={{0,4},{1,5},{2,6},{3,7},{4,8},{5,9},{6,10},{7,11},{8,12},{9,13},{1... | collective-permute-start | bytes 3145736 | tf_op jit(solution)/shard_map/ppermute | solution.py:17
  29.3 47.0 %collective-permute-start.1 = (bf16[256,2048]{1,0:T(8,128)(2,1)}, bf16[256,2048]{1,0:T(8,128)(2,1)S(1)}, u32[]{:S(2)}, u32[]{:S(2)}) collective-permute-start(bf16[256,2048]{1,0:T(8,128)(2,1)} %refs_4_), channel_id=1, source_target_pairs={{0,2},{1,3},{2,4},{3,5},{4,6},{5,7},{6,8},{7,9},{8,10},{9,11},{10,... | collective-permute-start | bytes 3145736 | tf_op jit(solution)/shard_map/ppermute | solution.py:17
  53.1 24.9 %copy-start.1 = (bf16[256,2048]{1,0:T(8,128)(2,1)}, bf16[256,2048]{1,0:T(8,128)(2,1)S(1)}, u32[]{:S(2)}) copy-start(bf16[256,2048]{1,0:T(8,128)(2,1)S(1)} %collective-permute-done.refs_0_) | copy-start | bytes 3145732
  76.3 1.8 %copy-start.2 = (bf16[256,2048]{1,0:T(8,128)(2,1)}, bf16[256,2048]{1,0:T(8,128)(2,1)S(1)}, u32[]{:S(2)}) copy-start(bf16[256,2048]{1,0:T(8,128)(2,1)S(1)} %collective-permute-done.1.refs_2_) | copy-start | bytes 3145732
  79.6 4.4 %collective-permute-start.2 = (bf16[2,256,2048]{2,1,0:T(8,128)(2,1)}, bf16[2,256,2048]{2,1,0:T(8,128)(2,1)S(1)}, u32[]{:S(2)}, u32[]{:S(2)}) collective-permute-start(bf16[2,256,2048]{2,1,0:T(8,128)(2,1)} %pad_maximum_fusion), channel_id=1, source_target_pairs={{0,1},{1,0},{2,3},{3,2},{4,5},{5,4},{6,7},{7,6},{8,9},{9,8},{10,11... | collective-permute-start | bytes 6291464 | tf_op jit(solution)/shard_map/ppermute | solution.py:109
  84.0 1.4 %copy-start = (bf16[2,256,2048]{2,1,0:T(8,128)(2,1)}, bf16[2,256,2048]{2,1,0:T(8,128)(2,1)S(1)}, u32[]{:S(2)}) copy-start(bf16[2,256,2048]{2,1,0:T(8,128)(2,1)S(1)} %collective-permute-done.2.refs_1_.refs_3_) | copy-start | bytes 6291460

commit v8 on v4

--- a/solution.py
+++ b/solution.py
@@ -9,6 +9,7 @@
 
 TILE = 128
 LANES = 128
+STEP = 64
 
 
 def from_behind(shard, axis, by):
@@ -30,24 +31,27 @@
     gate_ref, skip_ref, out_ref = refs[hops + 1:]
     block_rows = blocks[0].shape[0]
     groups_here = rows_ref.shape[0]
-    span = hops * block_rows + TILE
-    sub_tiles = span // TILE
-    out_tiles = block_rows // TILE
+    out_tiles = block_rows // STEP
+    span = hops * block_rows + STEP
+    col_blocks = -(-span // TILE)
+    width = col_blocks * TILE
     x = jnp.concatenate([b[...] for b in blocks], axis=0)
+    pad = (out_tiles - 1) * STEP + width - x.shape[0]
+    x = jnp.concatenate([x, jnp.zeros((pad, x.shape[1]), x.dtype)], axis=0)
     w = jnp.concatenate(
-        [x[i * TILE: i * TILE + span] for i in range(out_tiles)], axis=1)
-    lane_group = lax.broadcasted_iota(jnp.int32, (TILE, w.shape[1]), 1) % LANES // group_width
-    upper = (lax.broadcasted_iota(jnp.int32, (TILE, TILE), 1)
-             >= lax.broadcasted_iota(jnp.int32, (TILE, TILE), 0))
-    acc = jnp.zeros((TILE, w.shape[1]), jnp.float32)
+        [x[i * STEP: i * STEP + width] for i in range(out_tiles)], axis=1)
+    lane_group = lax.broadcasted_iota(jnp.int32, (STEP, w.shape[1]), 1) % LANES // group_width
+    upper = (lax.broadcasted_iota(jnp.int32, (STEP, TILE), 1)
+             >= lax.broadcasted_iota(jnp.int32, (STEP, TILE), 0))
+    acc = jnp.zeros((STEP, w.shape[1]), jnp.float32)
     for gg in range(groups_here):
         rolled = []
-        for k in range(sub_tiles + 1):
+        for k in range(col_blocks + 1):
             window = rows_ref[gg:gg + 1, k * TILE:(k + 1) * TILE]
-            window = jnp.broadcast_to(window, (TILE, TILE))
+            window = jnp.broadcast_to(window, (STEP, TILE))
             rolled.append(pltpu.roll(window, 0, 1, stride=1, stride_axis=0))
         toeplitz = jnp.concatenate(
-            [jnp.where(upper, rolled[k + 1], rolled[k]) for k in range(sub_tiles)],
+            [jnp.where(upper, rolled[k + 1], rolled[k]) for k in range(col_blocks)],
             axis=1).astype(jnp.bfloat16)
         part = jnp.dot(toeplitz, w, preferred_element_type=jnp.float32)
         acc = jnp.where(lane_group == gg, part, acc)

time: 97.4 us -> 109 us (1.12)
  Pallas kernels: 19.4 us -> 31.5 us
    pallas_call x1, Pallas kernels: 19.4 us -> 31.5 us  [convolve(): pl.pallas_call(kernel, grid=(chunks,), in_specs=[pl.BlockSpec((groups_per...]
where the time goes in v8:
time: 109 us; the launch traced here: 108 us
  waiting for transfers between devices  46.5 us (43%)
  Pallas kernels  31.5 us (29%)
  blocking collectives  19.8 us (18%)
  starting transfers between devices  3.84 us (4%)
  local copies, waits for them, and re-layouts  3.44 us (3%)
  other arithmetic  3.31 us (3%)
    ppermute x2, waiting for transfers between devices, from_behind(): return lax.ppermute(shard, axis, pairs)  44.2 us
    pallas_call x1, Pallas kernels, convolve(): pl.pallas_call(kernel, grid=(chunks,), in_specs=[pl.BlockSpec((groups_per...  31.5 us
    all_gather x1, blocking collectives, body(): all_taps = lax.all_gather(taps, 'seq', axis=0, tiled=True)  19.8 us
    ppermute x2, starting transfers between devices, from_behind(): return lax.ppermute(shard, axis, pairs)  3.83 us
    another operation x2, other arithmetic, body(): jnp.stack([jnp.where(first_core, signal, back_one), jnp.where(first_core,...  3.31 us
    ppermute x1, waiting for transfers between devices, body(): odd = lax.ppermute(outgoing, 'seq', swap)  2.26 us
  transfers between devices with their start and end apart: 3, of which 3 were waited for; matrix products, arithmetic and copies ran while one was open for 2% of the time, Pallas kernels for 0%

profile of v8, /device:TPU:8, one launch (start us, length us, event | category | flops | bytes accessed | tf_op | source)
XLA Modules:
  0.0 108.4 jit_solution(2695255343374166593)
XLA Ops:
  0.0 19.8 %all_gather.3 = bf16[1024,128]{1,0:T(8,128)(2,1)S(1)} all-gather(bf16[64,128]{1,0:T(8,128)(2,1)} %param.7), channel_id=1, replica_groups=mesh['rep'=2,'seq'=16] {'seq'}, dimensions={0}, use_global_device_ids=true | all-gather | bytes 278528 | tf_op jit(solution)/shard_map/all_gather | solution.py:97
  19.8 1.9 %collective-permute-start = (bf16[256,2048]{1,0:T(8,128)(2,1)}, bf16[256,2048]{1,0:T(8,128)(2,1)S(1)}, u32[]{:S(2)}, u32[]{:S(2)}) collective-permute-start(bf16[256,2048]{1,0:T(8,128)(2,1)} %refs_4_), channel_id=1, source_target_pairs={{0,4},{1,5},{2,6},{3,7},{4,8},{5,9},{6,10},{7,11},{8,12},{9,13},{1... | collective-permute-start | bytes 3145736 | tf_op jit(solution)/shard_map/ppermute | solution.py:18
  21.7 1.9 %collective-permute-start.1 = (bf16[256,2048]{1,0:T(8,128)(2,1)}, bf16[256,2048]{1,0:T(8,128)(2,1)S(1)}, u32[]{:S(2)}, u32[]{:S(2)}) collective-permute-start(bf16[256,2048]{1,0:T(8,128)(2,1)} %refs_4_), channel_id=1, source_target_pairs={{0,2},{1,3},{2,4},{3,5},{4,6},{5,7},{6,8},{7,9},{8,10},{9,11},{10,... | collective-permute-start | bytes 3145736 | tf_op jit(solution)/shard_map/ppermute | solution.py:18
  23.6 24.5 %collective-permute-done.refs_0_ = bf16[256,2048]{1,0:T(8,128)(2,1)S(1)} collective-permute-done((bf16[256,2048]{1,0:T(8,128)(2,1)}, bf16[256,2048]{1,0:T(8,128)(2,1)S(1)}, u32[]{:S(2)}, u32[]{:S(2)}) %collective-permute-start) | collective-permute-done | bytes 1048608 | tf_op jit(solution)/shard_map/ppermute | solution.py:18
  48.2 0.0 copy-start.1
  48.2 19.7 %collective-permute-done.1.refs_2_ = bf16[256,2048]{1,0:T(8,128)(2,1)S(1)} collective-permute-done((bf16[256,2048]{1,0:T(8,128)(2,1)}, bf16[256,2048]{1,0:T(8,128)(2,1)S(1)}, u32[]{:S(2)}, u32[]{:S(2)}) %collective-permute-start.1) | collective-permute-done | bytes 1048608 | tf_op jit(solution)/shard_map/ppermute | solution.py:18
  67.9 0.0 copy-start.2
  67.9 1.8 %select_bitcast_fusion.1 = (bf16[1,256,2048]{2,1,0:T(8,128)(2,1)S(1)}, bf16[1,256,2048]{2,1,0:T(8,128)(2,1)S(1)}) fusion(bf16[256,2048]{1,0:T(8,128)(2,1)} %refs_4_, bf16[256,2048]{1,0:T(8,128)(2,1)S(1)} %collective-permute-done.1.refs_2_, pred[]{:T(512)S(6)} %eq.5, bf16[256,2048]{1,0:T(8,128)(2,1)S(1)} %collective-permute-done.refs_0_), kind=kLoop, calls=%fused_computation.2 | loop fusion | flops 1048576 | bytes 5242881 | tf_op jit(solution)/shard_map/stack | solution.py:108
  69.6 0.0 copy-done.1
  69.7 0.0 copy-done.2
  69.7 1.5 %pad_maximum_fusion = bf16[2,256,2048]{2,1,0:T(8,128)(2,1)} fusion(bf16[1,256,2048]{2,1,0:T(8,128)(2,1)S(1)} %get-tuple-element.10, bf16[1,256,2048]{2,1,0:T(8,128)(2,1)S(1)} %get-tuple-element.9), kind=kLoop, calls=%fused_computation | loop fusion | flops 1048576 | bytes 4194304 | tf_op jit(solution)/shard_map/stack | solution.py:108
  71.2 0.0 collective-permute-start.2
  71.2 0.1 copy.6
  71.4 0.8 rev.3
  72.2 1.1 concatenate.3.rows_ref
  73.3 2.3 %collective-permute-done.2.refs_1_.refs_3_ = bf16[2,256,2048]{2,1,0:T(8,128)(2,1)S(1)} collective-permute-done((bf16[2,256,2048]{2,1,0:T(8,128)(2,1)}, bf16[2,256,2048]{2,1,0:T(8,128)(2,1)S(1)}, u32[]{:S(2)}, u32[]{:S(2)}) %collective-permute-start.2) | collective-permute-done | bytes 2097184 | tf_op jit(solution)/shard_map/ppermute | solution.py:112
  75.6 0.0 copy-start
  75.6 1.4 %copy-done = bf16[2,256,2048]{2,1,0:T(8,128)(2,1)} copy-done((bf16[2,256,2048]{2,1,0:T(8,128)(2,1)}, bf16[2,256,2048]{2,1,0:T(8,128)(2,1)S(1)}, u32[]{:S(2)}) %copy-start) | copy-done | bytes 2097176
  76.9 31.5 %shard_map.46 = bf16[256,2048]{1,0:T(8,128)(2,1)} custom-call(f32[128,1280]{1,0:T(8,128)} %concatenate.3.rows_ref, bf16[256,2048]{1,0:T(8,128)(2,1)} %copy-done.1, bf16[2,256,2048]{2,1,0:T(8,128)(2,1)} %copy-done, bf16[256,2048]{1,0:T(8,128)(2,1)} %copy-done.2, bf16[2,256,2048]{2,1,0:T(8,128)(2,1)} %copy-done, bf16[256,2048]{1,0:T(8,128)(2,1)} %refs_4_, ...), custom_call_target="tpu_custom_call" | custom-call | tf_op jit(solution)/shard_map/pallas_call | solution.py:81
  (2 shorter events, 0.0 us)
Async XLA Ops:
  19.8 28.4 %collective-permute-start = (bf16[256,2048]{1,0:T(8,128)(2,1)}, bf16[256,2048]{1,0:T(8,128)(2,1)S(1)}, u32[]{:S(2)}, u32[]{:S(2)}) collective-permute-start(bf16[256,2048]{1,0:T(8,128)(2,1)} %refs_4_), channel_id=1, source_target_pairs={{0,4},{1,5},{2,6},{3,7},{4,8},{5,9},{6,10},{7,11},{8,12},{9,13},{1... | collective-permute-start | bytes 3145736 | tf_op jit(solution)/shard_map/ppermute | solution.py:18
  21.7 46.2 %collective-permute-start.1 = (bf16[256,2048]{1,0:T(8,128)(2,1)}, bf16[256,2048]{1,0:T(8,128)(2,1)S(1)}, u32[]{:S(2)}, u32[]{:S(2)}) collective-permute-start(bf16[256,2048]{1,0:T(8,128)(2,1)} %refs_4_), channel_id=1, source_target_pairs={{0,2},{1,3},{2,4},{3,5},{4,6},{5,7},{6,8},{7,9},{8,10},{9,11},{10,... | collective-permute-start | bytes 3145736 | tf_op jit(solution)/shard_map/ppermute | solution.py:18
  48.2 21.5 %copy-start.1 = (bf16[256,2048]{1,0:T(8,128)(2,1)}, bf16[256,2048]{1,0:T(8,128)(2,1)S(1)}, u32[]{:S(2)}) copy-start(bf16[256,2048]{1,0:T(8,128)(2,1)S(1)} %collective-permute-done.refs_0_) | copy-start | bytes 3145732
  67.9 1.8 %copy-start.2 = (bf16[256,2048]{1,0:T(8,128)(2,1)}, bf16[256,2048]{1,0:T(8,128)(2,1)S(1)}, u32[]{:S(2)}) copy-start(bf16[256,2048]{1,0:T(8,128)(2,1)S(1)} %collective-permute-done.1.refs_2_) | copy-start | bytes 3145732
  71.2 4.4 %collective-permute-start.2 = (bf16[2,256,2048]{2,1,0:T(8,128)(2,1)}, bf16[2,256,2048]{2,1,0:T(8,128)(2,1)S(1)}, u32[]{:S(2)}, u32[]{:S(2)}) collective-permute-start(bf16[2,256,2048]{2,1,0:T(8,128)(2,1)} %pad_maximum_fusion), channel_id=1, source_target_pairs={{0,1},{1,0},{2,3},{3,2},{4,5},{5,4},{6,7},{7,6},{8,9},{9,8},{10,11... | collective-permute-start | bytes 6291464 | tf_op jit(solution)/shard_map/ppermute | solution.py:112
  75.6 1.4 %copy-start = (bf16[2,256,2048]{2,1,0:T(8,128)(2,1)}, bf16[2,256,2048]{2,1,0:T(8,128)(2,1)S(1)}, u32[]{:S(2)}) copy-start(bf16[2,256,2048]{2,1,0:T(8,128)(2,1)S(1)} %collective-permute-done.2.refs_1_.refs_3_) | copy-start | bytes 6291460

commit v9 on v4

--- a/solution.py
+++ b/solution.py
@@ -98,12 +98,26 @@
     if hops != 4 or lax.axis_size("seq") % 2:
         received = [from_behind(signal, "seq", d) for d in range(hops, 0, -1)]
         return convolve(rows, received + [signal], gate, skip, group_width)
-    back_one = from_behind(signal, "seq", 2)
-    back_two = from_behind(signal, "seq", 4)
+    count = lax.axis_size("seq")
+    if count % 4:
+        back_one = from_behind(signal, "seq", 2)
+        back_two = from_behind(signal, "seq", 4)
+    else:
+        half = block_rows // 2
+        first = from_behind(signal[:half], "seq", 4)
+        first, rest = lax.optimization_barrier((first, signal[half:]))
+        second = from_behind(rest, "seq", 4)
+        back_two = jnp.concatenate([first, second], axis=0)
+        up = [(i, i + 2) for i in range(count) if (i // 2) % 2 == 0]
+        down = [(i, i - 2) for i in range(count) if (i // 2) % 2 == 1]
+        direct = lax.ppermute(signal, "seq", up)
+        relayed = jnp.concatenate([lax.ppermute(first, "seq", down),
+                                   lax.ppermute(second, "seq", down)], axis=0)
+        odd_chip = (lax.axis_index("seq") // 2) % 2 == 1
+        back_one = jnp.where(odd_chip, direct, relayed)
     first_core = lax.axis_index("seq") % 2 == 0
     outgoing = jnp.stack([jnp.where(first_core, signal, back_one),
                           jnp.where(first_core, back_one, back_two)])
-    count = lax.axis_size("seq")
     swap = [(i, i ^ 1) for i in range(count)]
     odd = lax.ppermute(outgoing, "seq", swap)
     return convolve(rows, [back_two, (odd, 1), back_one, (odd, 0), signal],

time: 97.4 us -> 97.6 us (level)
  waiting for transfers between devices: 46.5 us -> 41.7 us
  starting transfers between devices: 3.84 us -> 7.76 us
    ppermute x2, waiting for transfers between devices: 44.2 us -> 25.9 us  [from_behind(): return lax.ppermute(shard, axis, pairs)]
    ppermute x0 -> x3, waiting for transfers between devices: none -> 13.4 us  [the longest x1 12.8 us: body(): lax.ppermute(second, 'seq', down)]
    ppermute x0 -> x3, starting transfers between devices: none -> 3.93 us  [the longest x1 1.36 us: body(): direct = lax.ppermute(signal, 'seq', up)]
    unnamed x6 -> x7, local copies, waits for them, and re-layouts: 1.36 us -> 0.05 us
    slice x0 -> x1, local copies, waits for them, and re-layouts: none -> 1.27 us  [body(): first, rest = lax.optimization_barrier((first, signal[half:]))]
    another operation x2 -> x3, other arithmetic: 3.31 us -> 3.45 us  [body(): jnp.stack([jnp.where(first_core, signal, back_one), jnp.where(first_core,...]
  transfers between devices with their start and end apart: 3 -> 6, of which waited for: 3 -> 5; matrix products, arithmetic and copies ran while one was open for 2% -> 2% of each run, Pallas kernels for 0% -> 0%
where the time goes in v9:
time: 97.6 us; the launch traced here: 95.8 us
  waiting for transfers between devices  41.7 us (43%)
  blocking collectives  19.9 us (20%)
  Pallas kernels  19.4 us (20%)
  starting transfers between devices  7.76 us (8%)
  other arithmetic  3.45 us (4%)
  local copies, waits for them, and re-layouts  3.43 us (4%)
    ppermute x2, waiting for transfers between devices, from_behind(): return lax.ppermute(shard, axis, pairs)  25.9 us
    all_gather x1, blocking collectives, body(): all_taps = lax.all_gather(taps, 'seq', axis=0, tiled=True)  19.9 us
    pallas_call x1, Pallas kernels, convolve(): pl.pallas_call(kernel, grid=(chunks,), in_specs=[pl.BlockSpec((groups_per...  19.4 us
    ppermute x1, waiting for transfers between devices, body(): lax.ppermute(second, 'seq', down)  12.8 us
    ppermute x2, starting transfers between devices, from_behind(): return lax.ppermute(shard, axis, pairs)  3.83 us
    another operation x3, other arithmetic, body(): jnp.stack([jnp.where(first_core, signal, back_one), jnp.where(first_core,...  3.45 us
    ppermute x1, waiting for transfers between devices, body(): odd = lax.ppermute(outgoing, 'seq', swap)  2.4 us
  transfers between devices with their start and end apart: 6, of which 5 were waited for; matrix products, arithmetic and copies ran while one was open for 2% of the time, Pallas kernels for 0%

profile of v9, /device:TPU:8, one launch (start us, length us, event | category | flops | bytes accessed | tf_op | source)
XLA Modules:
  0.0 95.8 jit_solution(9828006083349599093)
XLA Ops:
  0.0 0.0 copy-start
  0.0 19.9 %all_gather.3 = bf16[1024,128]{1,0:T(8,128)(2,1)S(1)} all-gather(bf16[64,128]{1,0:T(8,128)(2,1)} %param.7), channel_id=1, replica_groups=mesh['rep'=2,'seq'=16] {'seq'}, dimensions={0}, use_global_device_ids=true | all-gather | bytes 278528 | tf_op jit(solution)/shard_map/all_gather | solution.py:93
  19.9 1.3 %fusion = (bf16[128,2048]{1,0:T(8,128)(2,1)S(1)}, bf16[128,2048]{1,0:T(8,128)(2,1)S(1)}) fusion(bf16[256,2048]{1,0:T(8,128)(2,1)} %refs_4_), kind=kLoop, calls=%fused_computation.6 | loop fusion | bytes 2097152 | tf_op jit(solution)/shard_map/slice | solution.py:108
  21.2 1.9 %collective-permute-start = (bf16[128,2048]{1,0:T(8,128)(2,1)S(1)}, bf16[128,2048]{1,0:T(8,128)(2,1)S(1)}, u32[]{:S(2)}, u32[]{:S(2)}) collective-permute-start(bf16[128,2048]{1,0:T(8,128)(2,1)S(1)} %get-tuple-element.16), channel_id=1, source_target_pairs={{0,4},{1,5},{2,6},{3,7},{4,8},{5,9},{6,10},{7,11},{8,12},{9,13},{1... | collective-permute-start | bytes 1572872 | tf_op jit(solution)/shard_map/ppermute | solution.py:17
  23.1 0.0 copy-done
  23.1 1.4 %collective-permute-start.2 = (bf16[256,2048]{1,0:T(8,128)(2,1)S(1)}, bf16[256,2048]{1,0:T(8,128)(2,1)S(1)}, u32[]{:S(2)}, u32[]{:S(2)}) collective-permute-start(bf16[256,2048]{1,0:T(8,128)(2,1)S(1)} %copy-done), channel_id=1, source_target_pairs={{0,2},{1,3},{4,6},{5,7},{8,10},{9,11},{12,14},{13,15},{16,18},{17,... | collective-permute-start | bytes 3145736 | tf_op jit(solution)/shard_map/ppermute | solution.py:113
  24.5 13.7 %collective-permute-done = bf16[128,2048]{1,0:T(8,128)(2,1)S(1)} collective-permute-done((bf16[128,2048]{1,0:T(8,128)(2,1)S(1)}, bf16[128,2048]{1,0:T(8,128)(2,1)S(1)}, u32[]{:S(2)}, u32[]{:S(2)}) %collective-permute-start) | collective-permute-done | bytes 524320 | tf_op jit(solution)/shard_map/ppermute | solution.py:17
  38.1 1.9 %collective-permute-start.1 = (bf16[128,2048]{1,0:T(8,128)(2,1)S(1)}, bf16[128,2048]{1,0:T(8,128)(2,1)S(1)}, u32[]{:S(2)}, u32[]{:S(2)}) collective-permute-start(bf16[128,2048]{1,0:T(8,128)(2,1)S(1)} %get-tuple-element.12), channel_id=1, source_target_pairs={{0,4},{1,5},{2,6},{3,7},{4,8},{5,9},{6,10},{7,11},{8,12},{9,13},{1... | collective-permute-start | bytes 1572872 | tf_op jit(solution)/shard_map/ppermute | solution.py:17
  40.1 1.3 %collective-permute-start.3 = (bf16[128,2048]{1,0:T(8,128)(2,1)S(1)}, bf16[128,2048]{1,0:T(8,128)(2,1)}, u32[]{:S(2)}, u32[]{:S(2)}) collective-permute-start(bf16[128,2048]{1,0:T(8,128)(2,1)S(1)} %collective-permute-done), channel_id=1, source_target_pairs={{2,0},{3,1},{6,4},{7,5},{10,8},{11,9},{14,12},{15,13},{18,16},{19,... | collective-permute-start | bytes 1572872 | tf_op jit(solution)/shard_map/ppermute | solution.py:114
  41.4 12.3 %collective-permute-done.1 = bf16[128,2048]{1,0:T(8,128)(2,1)S(1)} collective-permute-done((bf16[128,2048]{1,0:T(8,128)(2,1)S(1)}, bf16[128,2048]{1,0:T(8,128)(2,1)S(1)}, u32[]{:S(2)}, u32[]{:S(2)}) %collective-permute-start.1) | collective-permute-done | bytes 524320 | tf_op jit(solution)/shard_map/ppermute | solution.py:17
  53.6 1.3 %collective-permute-start.4 = (bf16[128,2048]{1,0:T(8,128)(2,1)S(1)}, bf16[128,2048]{1,0:T(8,128)(2,1)}, u32[]{:S(2)}, u32[]{:S(2)}) collective-permute-start(bf16[128,2048]{1,0:T(8,128)(2,1)S(1)} %collective-permute-done.1), channel_id=1, source_target_pairs={{2,0},{3,1},{6,4},{7,5},{10,8},{11,9},{14,12},{15,13},{18,16},{19,... | collective-permute-start | bytes 1572872 | tf_op jit(solution)/shard_map/ppermute | solution.py:115
  55.1 0.0 copy-start.2
  55.1 0.6 collective-permute-done.3
  55.7 0.0 collective-permute-done.2
  55.7 12.8 %collective-permute-done.4 = bf16[128,2048]{1,0:T(8,128)(2,1)} collective-permute-done((bf16[128,2048]{1,0:T(8,128)(2,1)S(1)}, bf16[128,2048]{1,0:T(8,128)(2,1)}, u32[]{:S(2)}, u32[]{:S(2)}) %collective-permute-start.4) | collective-permute-done | bytes 524320 | tf_op jit(solution)/shard_map/ppermute | solution.py:115
  68.5 1.8 %select_bitcast_fusion.1 = (bf16[1,256,2048]{2,1,0:T(8,128)(2,1)S(1)}, bf16[256,2048]{1,0:T(8,128)(2,1)S(1)}) fusion(bf16[256,2048]{1,0:T(8,128)(2,1)S(1)} %copy-done, pred[]{:T(512)S(6)} %eq.9, bf16[256,2048]{1,0:T(8,128)(2,1)S(1)} %collective-permute-done.2, bf16[128,2048]{1,0:T(8,128)(2,1)} %collective-permute-done.4, ...), kind=kLoop, calls=%fused_computation.3 | loop fusion | flops 3145728 | bytes 5242882 | tf_op jit(solution)/shard_map/stack | solution.py:119
  70.3 0.0 copy-start.1
  70.3 0.0 copy-done.2
  70.3 0.1 select_bitcast_fusion
  70.4 1.5 %pad_maximum_fusion = bf16[2,256,2048]{2,1,0:T(8,128)(2,1)} fusion(bf16[1,256,2048]{2,1,0:T(8,128)(2,1)S(1)} %select_bitcast_fusion, bf16[1,256,2048]{2,1,0:T(8,128)(2,1)S(1)} %get-tuple-element.13), kind=kLoop, calls=%fused_computation | loop fusion | flops 1048576 | bytes 4194304 | tf_op jit(solution)/shard_map/stack | solution.py:119
  71.9 0.0 copy-done.1
  72.0 0.0 collective-permute-start.5
  72.0 0.1 copy.6
  72.1 0.8 rev.3
  73.0 1.1 %concatenate.9.rows_ref = f32[128,1280]{1,0:T(8,128)} concatenate(f32[128,129]{1,0:T(8,128)S(1)} %broadcast_in_dim.6, bf16[128,1024]{1,0:T(8,128)(2,1)S(1)} %rev.3, f32[128,127]{1,0:T(8,128)S(1)} %broadcast_in_dim.7), dimensions={1} | concatenate | bytes 1048576 | tf_op jit(solution)/shard_map/concatenate | solution.py:25
  74.1 2.4 %collective-permute-done.5.refs_1_.refs_3_ = bf16[2,256,2048]{2,1,0:T(8,128)(2,1)} collective-permute-done((bf16[2,256,2048]{2,1,0:T(8,128)(2,1)}, bf16[2,256,2048]{2,1,0:T(8,128)(2,1)}, u32[]{:S(2)}, u32[]{:S(2)}) %collective-permute-start.5) | collective-permute-done | bytes 2097184 | tf_op jit(solution)/shard_map/ppermute | solution.py:122
  76.5 19.4 %shard_map.46 = bf16[256,2048]{1,0:T(8,128)(2,1)} custom-call(f32[128,1280]{1,0:T(8,128)} %concatenate.9.rows_ref, bf16[256,2048]{1,0:T(8,128)(2,1)} %copy-done.2, bf16[2,256,2048]{2,1,0:T(8,128)(2,1)} %collective-permute-done.5.refs_1_.refs_3_, bf16[256,2048]{1,0:T(8,128)(2,1)} %copy-done.1, bf16[2,256,2048]{2,1,0:T(8,128)(2,1)} %collective-permute-done.5.refs_1_.refs_3_, ...), custom_call_target="tpu_custom_call" | custom-call | tf_op jit(solution)/shard_map/pallas_call | solution.py:77
  (4 shorter events, 0.1 us)
Async XLA Ops:
  0.0 23.1 %copy-start = (bf16[256,2048]{1,0:T(8,128)(2,1)S(1)}, bf16[256,2048]{1,0:T(8,128)(2,1)}, u32[]{:S(2)}) copy-start(bf16[256,2048]{1,0:T(8,128)(2,1)} %refs_4_) | copy-start | bytes 3145732
  21.2 17.0 %collective-permute-start = (bf16[128,2048]{1,0:T(8,128)(2,1)S(1)}, bf16[128,2048]{1,0:T(8,128)(2,1)S(1)}, u32[]{:S(2)}, u32[]{:S(2)}) collective-permute-start(bf16[128,2048]{1,0:T(8,128)(2,1)S(1)} %get-tuple-element.16), channel_id=1, source_target_pairs={{0,4},{1,5},{2,6},{3,7},{4,8},{5,9},{6,10},{7,11},{8,12},{9,13},{1... | collective-permute-start | bytes 1572872 | tf_op jit(solution)/shard_map/ppermute | solution.py:17
  23.1 32.5 %collective-permute-start.2 = (bf16[256,2048]{1,0:T(8,128)(2,1)S(1)}, bf16[256,2048]{1,0:T(8,128)(2,1)S(1)}, u32[]{:S(2)}, u32[]{:S(2)}) collective-permute-start(bf16[256,2048]{1,0:T(8,128)(2,1)S(1)} %copy-done), channel_id=1, source_target_pairs={{0,2},{1,3},{4,6},{5,7},{8,10},{9,11},{12,14},{13,15},{16,18},{17,... | collective-permute-start | bytes 3145736 | tf_op jit(solution)/shard_map/ppermute | solution.py:113
  38.1 15.5 %collective-permute-start.1 = (bf16[128,2048]{1,0:T(8,128)(2,1)S(1)}, bf16[128,2048]{1,0:T(8,128)(2,1)S(1)}, u32[]{:S(2)}, u32[]{:S(2)}) collective-permute-start(bf16[128,2048]{1,0:T(8,128)(2,1)S(1)} %get-tuple-element.12), channel_id=1, source_target_pairs={{0,4},{1,5},{2,6},{3,7},{4,8},{5,9},{6,10},{7,11},{8,12},{9,13},{1... | collective-permute-start | bytes 1572872 | tf_op jit(solution)/shard_map/ppermute | solution.py:17
  40.1 15.6 %collective-permute-start.3 = (bf16[128,2048]{1,0:T(8,128)(2,1)S(1)}, bf16[128,2048]{1,0:T(8,128)(2,1)}, u32[]{:S(2)}, u32[]{:S(2)}) collective-permute-start(bf16[128,2048]{1,0:T(8,128)(2,1)S(1)} %collective-permute-done), channel_id=1, source_target_pairs={{2,0},{3,1},{6,4},{7,5},{10,8},{11,9},{14,12},{15,13},{18,16},{19,... | collective-permute-start | bytes 1572872 | tf_op jit(solution)/shard_map/ppermute | solution.py:114
  53.6 14.8 %collective-permute-start.4 = (bf16[128,2048]{1,0:T(8,128)(2,1)S(1)}, bf16[128,2048]{1,0:T(8,128)(2,1)}, u32[]{:S(2)}, u32[]{:S(2)}) collective-permute-start(bf16[128,2048]{1,0:T(8,128)(2,1)S(1)} %collective-permute-done.1), channel_id=1, source_target_pairs={{2,0},{3,1},{6,4},{7,5},{10,8},{11,9},{14,12},{15,13},{18,16},{19,... | collective-permute-start | bytes 1572872 | tf_op jit(solution)/shard_map/ppermute | solution.py:115
  55.1 15.2 %copy-start.2 = (bf16[256,2048]{1,0:T(8,128)(2,1)}, bf16[256,2048]{1,0:T(8,128)(2,1)S(1)}, u32[]{:S(2)}) copy-start(bf16[256,2048]{1,0:T(8,128)(2,1)S(1)} %constant_dynamic-update-slice_fusion.refs_0_) | copy-start | bytes 3145732
  70.3 1.7 %copy-start.1 = (bf16[256,2048]{1,0:T(8,128)(2,1)}, bf16[256,2048]{1,0:T(8,128)(2,1)S(1)}, u32[]{:S(2)}) copy-start(bf16[256,2048]{1,0:T(8,128)(2,1)S(1)} %get-tuple-element.14.refs_2_) | copy-start | bytes 3145732
  72.0 4.5 %collective-permute-start.5 = (bf16[2,256,2048]{2,1,0:T(8,128)(2,1)}, bf16[2,256,2048]{2,1,0:T(8,128)(2,1)}, u32[]{:S(2)}, u32[]{:S(2)}) collective-permute-start(bf16[2,256,2048]{2,1,0:T(8,128)(2,1)} %pad_maximum_fusion), channel_id=1, source_target_pairs={{0,1},{1,0},{2,3},{3,2},{4,5},{5,4},{6,7},{7,6},{8,9},{9,8},{10,11... | collective-permute-start | bytes 6291464 | tf_op jit(solution)/shard_map/ppermute | solution.py:122

commit v10 on v4

--- a/solution.py
+++ b/solution.py
@@ -29,46 +29,50 @@
     blocks = refs[:hops + 1]
     gate_ref, skip_ref, out_ref = refs[hops + 1:]
     block_rows = blocks[0].shape[0]
-    groups_here = rows_ref.shape[0]
+    groups_here = LANES // group_width
     span = hops * block_rows + TILE
     sub_tiles = span // TILE
     out_tiles = block_rows // TILE
-    x = jnp.concatenate([b[...] for b in blocks], axis=0)
-    w = jnp.concatenate(
-        [x[i * TILE: i * TILE + span] for i in range(out_tiles)], axis=1)
-    lane_group = lax.broadcasted_iota(jnp.int32, (TILE, w.shape[1]), 1) % LANES // group_width
     upper = (lax.broadcasted_iota(jnp.int32, (TILE, TILE), 1)
              >= lax.broadcasted_iota(jnp.int32, (TILE, TILE), 0))
-    acc = jnp.zeros((TILE, w.shape[1]), jnp.float32)
-    for gg in range(groups_here):
-        rolled = []
-        for k in range(sub_tiles + 1):
-            window = rows_ref[gg:gg + 1, k * TILE:(k + 1) * TILE]
-            window = jnp.broadcast_to(window, (TILE, TILE))
-            rolled.append(pltpu.roll(window, 0, 1, stride=1, stride_axis=0))
-        toeplitz = jnp.concatenate(
-            [jnp.where(upper, rolled[k + 1], rolled[k]) for k in range(sub_tiles)],
-            axis=1).astype(jnp.bfloat16)
-        part = jnp.dot(toeplitz, w, preferred_element_type=jnp.float32)
-        acc = jnp.where(lane_group == gg, part, acc)
-    conv = jnp.concatenate(
-        [acc[:, i * LANES:(i + 1) * LANES] for i in range(out_tiles)], axis=0)
-    cur = blocks[hops][...].astype(jnp.float32)
-    mixed = gate_ref[...].astype(jnp.float32) * (conv + skip_ref[...] * cur)
-    out_ref[...] = mixed.astype(out_ref.dtype)
+    lane_group = lax.broadcasted_iota(jnp.int32, (TILE, out_tiles * LANES), 1) % LANES // group_width
+    for sub in range(blocks[0].shape[1] // LANES):
+        lanes = slice(sub * LANES, (sub + 1) * LANES)
+        x = jnp.concatenate([b[:, lanes] for b in blocks], axis=0)
+        w = jnp.concatenate(
+            [x[i * TILE: i * TILE + span] for i in range(out_tiles)], axis=1)
+        acc = jnp.zeros((TILE, w.shape[1]), jnp.float32)
+        for gg in range(groups_here):
+            row = sub * groups_here + gg
+            rolled = []
+            for k in range(sub_tiles + 1):
+                window = rows_ref[row:row + 1, k * TILE:(k + 1) * TILE]
+                window = jnp.broadcast_to(window, (TILE, TILE))
+                rolled.append(pltpu.roll(window, 0, 1, stride=1, stride_axis=0))
+            toeplitz = jnp.concatenate(
+                [jnp.where(upper, rolled[k + 1], rolled[k]) for k in range(sub_tiles)],
+                axis=1).astype(jnp.bfloat16)
+            part = jnp.dot(toeplitz, w, preferred_element_type=jnp.float32)
+            acc = jnp.where(lane_group == gg, part, acc)
+        conv = jnp.concatenate(
+            [acc[:, i * LANES:(i + 1) * LANES] for i in range(out_tiles)], axis=0)
+        cur = blocks[hops][:, lanes].astype(jnp.float32)
+        mixed = gate_ref[:, lanes].astype(jnp.float32) * (conv + skip_ref[:, lanes] * cur)
+        out_ref[:, lanes] = mixed.astype(out_ref.dtype)
 
 
 def convolve(rows, blocks, gate, skip, group_width):
     hops = len(blocks) - 1
     block_rows, channels = gate.shape
-    chunks = channels // LANES
-    groups_per = LANES // group_width
-    block_spec = pl.BlockSpec((block_rows, LANES), lambda c: (0, c))
+    width = 2 * LANES if channels % (2 * LANES) == 0 else LANES
+    chunks = channels // width
+    groups_per = width // group_width
+    block_spec = pl.BlockSpec((block_rows, width), lambda c: (0, c))
     arrays, specs = [], []
     for block in blocks:
         if isinstance(block, tuple):
             arrays.append(block[0])
-            specs.append(pl.BlockSpec((None, block_rows, LANES),
+            specs.append(pl.BlockSpec((None, block_rows, width),
                                       lambda c, slot=block[1]: (slot, 0, c)))
         else:
             arrays.append(block)
@@ -79,7 +83,7 @@
         grid=(chunks,),
         in_specs=[pl.BlockSpec((groups_per, rows.shape[1]), lambda c: (c, 0))]
         + specs
-        + [block_spec, pl.BlockSpec((1, LANES), lambda c: (0, c))],
+        + [block_spec, pl.BlockSpec((1, width), lambda c: (0, c))],
         out_specs=block_spec,
         out_shape=jax.ShapeDtypeStruct(gate.shape, gate.dtype),
         compiler_params=pltpu.CompilerParams(dimension_semantics=("arbitrary",)),

time: 97.4 us -> 95.2 us (0.977)
  Pallas kernels: 19.4 us -> 17.5 us
    pallas_call x1, Pallas kernels: 19.4 us -> 17.5 us  [convolve(): pl.pallas_call(kernel, grid=(chunks,), in_specs=[pl.BlockSpec((groups_per...]
where the time goes in v10:
time: 95.2 us; the launch traced here: 94.4 us
  waiting for transfers between devices  46.5 us (49%)
  blocking collectives  19.8 us (21%)
  Pallas kernels  17.5 us (18%)
  starting transfers between devices  3.84 us (4%)
  local copies, waits for them, and re-layouts  3.44 us (4%)
  other arithmetic  3.31 us (3%)
    ppermute x2, waiting for transfers between devices, from_behind(): return lax.ppermute(shard, axis, pairs)  44.2 us
    all_gather x1, blocking collectives, body(): all_taps = lax.all_gather(taps, 'seq', axis=0, tiled=True)  19.8 us
    pallas_call x1, Pallas kernels, convolve(): pl.pallas_call(kernel, grid=(chunks,), in_specs=[pl.BlockSpec((groups_per...  17.5 us
    ppermute x2, starting transfers between devices, from_behind(): return lax.ppermute(shard, axis, pairs)  3.83 us
    another operation x2, other arithmetic, body(): jnp.stack([jnp.where(first_core, signal, back_one), jnp.where(first_core,...  3.31 us
    ppermute x1, waiting for transfers between devices, body(): odd = lax.ppermute(outgoing, 'seq', swap)  2.26 us
  transfers between devices with their start and end apart: 3, of which 3 were waited for; matrix products, arithmetic and copies ran while one was open for 2% of the time, Pallas kernels for 0%

profile of v10, /device:TPU:8, one launch (start us, length us, event | category | flops | bytes accessed | tf_op | source)
XLA Modules:
  0.0 94.4 jit_solution(6865050359955075347)
XLA Ops:
  0.0 19.8 %all_gather.3 = bf16[1024,128]{1,0:T(8,128)(2,1)S(1)} all-gather(bf16[64,128]{1,0:T(8,128)(2,1)} %param.7), channel_id=1, replica_groups=mesh['rep'=2,'seq'=16] {'seq'}, dimensions={0}, use_global_device_ids=true | all-gather | bytes 278528 | tf_op jit(solution)/shard_map/all_gather | solution.py:97
  19.8 1.9 %collective-permute-start = (bf16[256,2048]{1,0:T(8,128)(2,1)}, bf16[256,2048]{1,0:T(8,128)(2,1)S(1)}, u32[]{:S(2)}, u32[]{:S(2)}) collective-permute-start(bf16[256,2048]{1,0:T(8,128)(2,1)} %refs_4_), channel_id=1, source_target_pairs={{0,4},{1,5},{2,6},{3,7},{4,8},{5,9},{6,10},{7,11},{8,12},{9,13},{1... | collective-permute-start | bytes 3145736 | tf_op jit(solution)/shard_map/ppermute | solution.py:17
  21.7 1.9 %collective-permute-start.1 = (bf16[256,2048]{1,0:T(8,128)(2,1)}, bf16[256,2048]{1,0:T(8,128)(2,1)S(1)}, u32[]{:S(2)}, u32[]{:S(2)}) collective-permute-start(bf16[256,2048]{1,0:T(8,128)(2,1)} %refs_4_), channel_id=1, source_target_pairs={{0,2},{1,3},{2,4},{3,5},{4,6},{5,7},{6,8},{7,9},{8,10},{9,11},{10,... | collective-permute-start | bytes 3145736 | tf_op jit(solution)/shard_map/ppermute | solution.py:17
  23.6 24.5 %collective-permute-done.refs_0_ = bf16[256,2048]{1,0:T(8,128)(2,1)S(1)} collective-permute-done((bf16[256,2048]{1,0:T(8,128)(2,1)}, bf16[256,2048]{1,0:T(8,128)(2,1)S(1)}, u32[]{:S(2)}, u32[]{:S(2)}) %collective-permute-start) | collective-permute-done | bytes 1048608 | tf_op jit(solution)/shard_map/ppermute | solution.py:17
  48.2 0.0 copy-start.1
  48.2 19.7 %collective-permute-done.1.refs_2_ = bf16[256,2048]{1,0:T(8,128)(2,1)S(1)} collective-permute-done((bf16[256,2048]{1,0:T(8,128)(2,1)}, bf16[256,2048]{1,0:T(8,128)(2,1)S(1)}, u32[]{:S(2)}, u32[]{:S(2)}) %collective-permute-start.1) | collective-permute-done | bytes 1048608 | tf_op jit(solution)/shard_map/ppermute | solution.py:17
  67.9 0.0 copy-start.2
  67.9 1.8 %select_bitcast_fusion.1 = (bf16[1,256,2048]{2,1,0:T(8,128)(2,1)S(1)}, bf16[1,256,2048]{2,1,0:T(8,128)(2,1)S(1)}) fusion(bf16[256,2048]{1,0:T(8,128)(2,1)} %refs_4_, bf16[256,2048]{1,0:T(8,128)(2,1)S(1)} %collective-permute-done.1.refs_2_, pred[]{:T(512)S(6)} %eq.5, bf16[256,2048]{1,0:T(8,128)(2,1)S(1)} %collective-permute-done.refs_0_), kind=kLoop, calls=%fused_computation.2 | loop fusion | flops 1048576 | bytes 5242881 | tf_op jit(solution)/shard_map/stack | solution.py:108
  69.6 0.0 copy-done.1
  69.7 0.0 copy-done.2
  69.7 1.5 %pad_maximum_fusion = bf16[2,256,2048]{2,1,0:T(8,128)(2,1)} fusion(bf16[1,256,2048]{2,1,0:T(8,128)(2,1)S(1)} %get-tuple-element.10, bf16[1,256,2048]{2,1,0:T(8,128)(2,1)S(1)} %get-tuple-element.9), kind=kLoop, calls=%fused_computation | loop fusion | flops 1048576 | bytes 4194304 | tf_op jit(solution)/shard_map/stack | solution.py:108
  71.2 0.0 collective-permute-start.2
  71.2 0.1 copy.6
  71.4 0.8 rev.3
  72.2 1.1 %concatenate.3.rows_ref = f32[128,1280]{1,0:T(8,128)} concatenate(f32[128,129]{1,0:T(8,128)S(1)} %broadcast_in_dim.6, bf16[128,1024]{1,0:T(8,128)(2,1)S(1)} %rev.3, f32[128,127]{1,0:T(8,128)S(1)} %broadcast_in_dim.7), dimensions={1} | concatenate | bytes 1048576 | tf_op jit(solution)/shard_map/concatenate | solution.py:25
  73.3 2.3 %collective-permute-done.2.refs_1_.refs_3_ = bf16[2,256,2048]{2,1,0:T(8,128)(2,1)S(1)} collective-permute-done((bf16[2,256,2048]{2,1,0:T(8,128)(2,1)}, bf16[2,256,2048]{2,1,0:T(8,128)(2,1)S(1)}, u32[]{:S(2)}, u32[]{:S(2)}) %collective-permute-start.2) | collective-permute-done | bytes 2097184 | tf_op jit(solution)/shard_map/ppermute | solution.py:112
  75.6 0.0 copy-start
  75.6 1.4 %copy-done = bf16[2,256,2048]{2,1,0:T(8,128)(2,1)} copy-done((bf16[2,256,2048]{2,1,0:T(8,128)(2,1)}, bf16[2,256,2048]{2,1,0:T(8,128)(2,1)S(1)}, u32[]{:S(2)}) %copy-start) | copy-done | bytes 2097176
  76.9 17.5 %shard_map.46 = bf16[256,2048]{1,0:T(8,128)(2,1)} custom-call(f32[128,1280]{1,0:T(8,128)} %concatenate.3.rows_ref, bf16[256,2048]{1,0:T(8,128)(2,1)} %copy-done.1, bf16[2,256,2048]{2,1,0:T(8,128)(2,1)} %copy-done, bf16[256,2048]{1,0:T(8,128)(2,1)} %copy-done.2, bf16[2,256,2048]{2,1,0:T(8,128)(2,1)} %copy-done, bf16[256,2048]{1,0:T(8,128)(2,1)} %refs_4_, ...), custom_call_target="tpu_custom_call" | custom-call | tf_op jit(solution)/shard_map/pallas_call | solution.py:81
  (2 shorter events, 0.0 us)
Async XLA Ops:
  19.8 28.4 %collective-permute-start = (bf16[256,2048]{1,0:T(8,128)(2,1)}, bf16[256,2048]{1,0:T(8,128)(2,1)S(1)}, u32[]{:S(2)}, u32[]{:S(2)}) collective-permute-start(bf16[256,2048]{1,0:T(8,128)(2,1)} %refs_4_), channel_id=1, source_target_pairs={{0,4},{1,5},{2,6},{3,7},{4,8},{5,9},{6,10},{7,11},{8,12},{9,13},{1... | collective-permute-start | bytes 3145736 | tf_op jit(solution)/shard_map/ppermute | solution.py:17
  21.7 46.2 %collective-permute-start.1 = (bf16[256,2048]{1,0:T(8,128)(2,1)}, bf16[256,2048]{1,0:T(8,128)(2,1)S(1)}, u32[]{:S(2)}, u32[]{:S(2)}) collective-permute-start(bf16[256,2048]{1,0:T(8,128)(2,1)} %refs_4_), channel_id=1, source_target_pairs={{0,2},{1,3},{2,4},{3,5},{4,6},{5,7},{6,8},{7,9},{8,10},{9,11},{10,... | collective-permute-start | bytes 3145736 | tf_op jit(solution)/shard_map/ppermute | solution.py:17
  48.2 21.5 %copy-start.1 = (bf16[256,2048]{1,0:T(8,128)(2,1)}, bf16[256,2048]{1,0:T(8,128)(2,1)S(1)}, u32[]{:S(2)}) copy-start(bf16[256,2048]{1,0:T(8,128)(2,1)S(1)} %collective-permute-done.refs_0_) | copy-start | bytes 3145732
  67.9 1.8 %copy-start.2 = (bf16[256,2048]{1,0:T(8,128)(2,1)}, bf16[256,2048]{1,0:T(8,128)(2,1)S(1)}, u32[]{:S(2)}) copy-start(bf16[256,2048]{1,0:T(8,128)(2,1)S(1)} %collective-permute-done.1.refs_2_) | copy-start | bytes 3145732
  71.2 4.4 %collective-permute-start.2 = (bf16[2,256,2048]{2,1,0:T(8,128)(2,1)}, bf16[2,256,2048]{2,1,0:T(8,128)(2,1)S(1)}, u32[]{:S(2)}, u32[]{:S(2)}) collective-permute-start(bf16[2,256,2048]{2,1,0:T(8,128)(2,1)} %pad_maximum_fusion), channel_id=1, source_target_pairs={{0,1},{1,0},{2,3},{3,2},{4,5},{5,4},{6,7},{7,6},{8,9},{9,8},{10,11... | collective-permute-start | bytes 6291464 | tf_op jit(solution)/shard_map/ppermute | solution.py:112
  75.6 1.4 %copy-start = (bf16[2,256,2048]{2,1,0:T(8,128)(2,1)}, bf16[2,256,2048]{2,1,0:T(8,128)(2,1)S(1)}, u32[]{:S(2)}) copy-start(bf16[2,256,2048]{2,1,0:T(8,128)(2,1)S(1)} %collective-permute-done.2.refs_1_.refs_3_) | copy-start | bytes 6291460

commit v11 on v10

--- a/solution.py
+++ b/solution.py
@@ -64,7 +64,8 @@
 def convolve(rows, blocks, gate, skip, group_width):
     hops = len(blocks) - 1
     block_rows, channels = gate.shape
-    width = 2 * LANES if channels % (2 * LANES) == 0 else LANES
+    subs = next(n for n in (4, 2, 1) if channels % (n * LANES) == 0)
+    width = subs * LANES
     chunks = channels // width
     groups_per = width // group_width
     block_spec = pl.BlockSpec((block_rows, width), lambda c: (0, c))

time: 95.2 us -> 94.3 us (level)
  no operation moved by 1% of the time
where the time goes in v11:
time: 94.3 us; the launch traced here: 93.6 us
  waiting for transfers between devices  46.5 us (49%)
  blocking collectives  19.8 us (21%)
  Pallas kernels  16.7 us (18%)
  starting transfers between devices  3.84 us (4%)
  local copies, waits for them, and re-layouts  3.44 us (4%)
  other arithmetic  3.31 us (4%)
    ppermute x2, waiting for transfers between devices, from_behind(): return lax.ppermute(shard, axis, pairs)  44.2 us
    all_gather x1, blocking collectives, body(): all_taps = lax.all_gather(taps, 'seq', axis=0, tiled=True)  19.8 us
    pallas_call x1, Pallas kernels, convolve(): pl.pallas_call(kernel, grid=(chunks,), in_specs=[pl.BlockSpec((groups_per...  16.7 us
    ppermute x2, starting transfers between devices, from_behind(): return lax.ppermute(shard, axis, pairs)  3.83 us
    another operation x2, other arithmetic, body(): jnp.stack([jnp.where(first_core, signal, back_one), jnp.where(first_core,...  3.31 us
    ppermute x1, waiting for transfers between devices, body(): odd = lax.ppermute(outgoing, 'seq', swap)  2.26 us
  transfers between devices with their start and end apart: 3, of which 3 were waited for; matrix products, arithmetic and copies ran while one was open for 2% of the time, Pallas kernels for 0%

profile of v11, /device:TPU:8, one launch (start us, length us, event | category | flops | bytes accessed | tf_op | source)
XLA Modules:
  0.0 93.6 jit_solution(17993559757277547971)
XLA Ops:
  0.0 19.8 %all_gather.3 = bf16[1024,128]{1,0:T(8,128)(2,1)S(1)} all-gather(bf16[64,128]{1,0:T(8,128)(2,1)} %param.7), channel_id=1, replica_groups=mesh['rep'=2,'seq'=16] {'seq'}, dimensions={0}, use_global_device_ids=true | all-gather | bytes 278528 | tf_op jit(solution)/shard_map/all_gather | solution.py:98
  19.8 1.9 %collective-permute-start = (bf16[256,2048]{1,0:T(8,128)(2,1)}, bf16[256,2048]{1,0:T(8,128)(2,1)S(1)}, u32[]{:S(2)}, u32[]{:S(2)}) collective-permute-start(bf16[256,2048]{1,0:T(8,128)(2,1)} %refs_4_), channel_id=1, source_target_pairs={{0,4},{1,5},{2,6},{3,7},{4,8},{5,9},{6,10},{7,11},{8,12},{9,13},{1... | collective-permute-start | bytes 3145736 | tf_op jit(solution)/shard_map/ppermute | solution.py:17
  21.7 1.9 %collective-permute-start.1 = (bf16[256,2048]{1,0:T(8,128)(2,1)}, bf16[256,2048]{1,0:T(8,128)(2,1)S(1)}, u32[]{:S(2)}, u32[]{:S(2)}) collective-permute-start(bf16[256,2048]{1,0:T(8,128)(2,1)} %refs_4_), channel_id=1, source_target_pairs={{0,2},{1,3},{2,4},{3,5},{4,6},{5,7},{6,8},{7,9},{8,10},{9,11},{10,... | collective-permute-start | bytes 3145736 | tf_op jit(solution)/shard_map/ppermute | solution.py:17
  23.6 24.5 %collective-permute-done.refs_0_ = bf16[256,2048]{1,0:T(8,128)(2,1)S(1)} collective-permute-done((bf16[256,2048]{1,0:T(8,128)(2,1)}, bf16[256,2048]{1,0:T(8,128)(2,1)S(1)}, u32[]{:S(2)}, u32[]{:S(2)}) %collective-permute-start) | collective-permute-done | bytes 1048608 | tf_op jit(solution)/shard_map/ppermute | solution.py:17
  48.2 0.0 copy-start.1
  48.2 19.7 %collective-permute-done.1.refs_2_ = bf16[256,2048]{1,0:T(8,128)(2,1)S(1)} collective-permute-done((bf16[256,2048]{1,0:T(8,128)(2,1)}, bf16[256,2048]{1,0:T(8,128)(2,1)S(1)}, u32[]{:S(2)}, u32[]{:S(2)}) %collective-permute-start.1) | collective-permute-done | bytes 1048608 | tf_op jit(solution)/shard_map/ppermute | solution.py:17
  67.9 0.0 copy-start.2
  67.9 1.8 %select_bitcast_fusion.1 = (bf16[1,256,2048]{2,1,0:T(8,128)(2,1)S(1)}, bf16[1,256,2048]{2,1,0:T(8,128)(2,1)S(1)}) fusion(bf16[256,2048]{1,0:T(8,128)(2,1)} %refs_4_, bf16[256,2048]{1,0:T(8,128)(2,1)S(1)} %collective-permute-done.1.refs_2_, pred[]{:T(512)S(6)} %eq.5, bf16[256,2048]{1,0:T(8,128)(2,1)S(1)} %collective-permute-done.refs_0_), kind=kLoop, calls=%fused_computation.2 | loop fusion | flops 1048576 | bytes 5242881 | tf_op jit(solution)/shard_map/stack | solution.py:109
  69.6 0.0 copy-done.1
  69.7 0.0 copy-done.2
  69.7 1.5 %pad_maximum_fusion = bf16[2,256,2048]{2,1,0:T(8,128)(2,1)} fusion(bf16[1,256,2048]{2,1,0:T(8,128)(2,1)S(1)} %get-tuple-element.10, bf16[1,256,2048]{2,1,0:T(8,128)(2,1)S(1)} %get-tuple-element.9), kind=kLoop, calls=%fused_computation | loop fusion | flops 1048576 | bytes 4194304 | tf_op jit(solution)/shard_map/stack | solution.py:109
  71.2 0.0 collective-permute-start.2
  71.2 0.1 copy.6
  71.4 0.8 rev.3
  72.2 1.1 %concatenate.3.rows_ref = f32[128,1280]{1,0:T(8,128)} concatenate(f32[128,129]{1,0:T(8,128)S(1)} %broadcast_in_dim.6, bf16[128,1024]{1,0:T(8,128)(2,1)S(1)} %rev.3, f32[128,127]{1,0:T(8,128)S(1)} %broadcast_in_dim.7), dimensions={1} | concatenate | bytes 1048576 | tf_op jit(solution)/shard_map/concatenate | solution.py:25
  73.3 2.3 %collective-permute-done.2.refs_1_.refs_3_ = bf16[2,256,2048]{2,1,0:T(8,128)(2,1)S(1)} collective-permute-done((bf16[2,256,2048]{2,1,0:T(8,128)(2,1)}, bf16[2,256,2048]{2,1,0:T(8,128)(2,1)S(1)}, u32[]{:S(2)}, u32[]{:S(2)}) %collective-permute-start.2) | collective-permute-done | bytes 2097184 | tf_op jit(solution)/shard_map/ppermute | solution.py:113
  75.6 0.0 copy-start
  75.6 1.4 %copy-done = bf16[2,256,2048]{2,1,0:T(8,128)(2,1)} copy-done((bf16[2,256,2048]{2,1,0:T(8,128)(2,1)}, bf16[2,256,2048]{2,1,0:T(8,128)(2,1)S(1)}, u32[]{:S(2)}) %copy-start) | copy-done | bytes 2097176
  76.9 16.7 %shard_map.46 = bf16[256,2048]{1,0:T(8,128)(2,1)} custom-call(f32[128,1280]{1,0:T(8,128)} %concatenate.3.rows_ref, bf16[256,2048]{1,0:T(8,128)(2,1)} %copy-done.1, bf16[2,256,2048]{2,1,0:T(8,128)(2,1)} %copy-done, bf16[256,2048]{1,0:T(8,128)(2,1)} %copy-done.2, bf16[2,256,2048]{2,1,0:T(8,128)(2,1)} %copy-done, bf16[256,2048]{1,0:T(8,128)(2,1)} %refs_4_, ...), custom_call_target="tpu_custom_call" | custom-call | tf_op jit(solution)/shard_map/pallas_call | solution.py:82
  (2 shorter events, 0.0 us)
Async XLA Ops:
  19.8 28.4 %collective-permute-start = (bf16[256,2048]{1,0:T(8,128)(2,1)}, bf16[256,2048]{1,0:T(8,128)(2,1)S(1)}, u32[]{:S(2)}, u32[]{:S(2)}) collective-permute-start(bf16[256,2048]{1,0:T(8,128)(2,1)} %refs_4_), channel_id=1, source_target_pairs={{0,4},{1,5},{2,6},{3,7},{4,8},{5,9},{6,10},{7,11},{8,12},{9,13},{1... | collective-permute-start | bytes 3145736 | tf_op jit(solution)/shard_map/ppermute | solution.py:17
  21.7 46.2 %collective-permute-start.1 = (bf16[256,2048]{1,0:T(8,128)(2,1)}, bf16[256,2048]{1,0:T(8,128)(2,1)S(1)}, u32[]{:S(2)}, u32[]{:S(2)}) collective-permute-start(bf16[256,2048]{1,0:T(8,128)(2,1)} %refs_4_), channel_id=1, source_target_pairs={{0,2},{1,3},{2,4},{3,5},{4,6},{5,7},{6,8},{7,9},{8,10},{9,11},{10,... | collective-permute-start | bytes 3145736 | tf_op jit(solution)/shard_map/ppermute | solution.py:17
  48.2 21.5 %copy-start.1 = (bf16[256,2048]{1,0:T(8,128)(2,1)}, bf16[256,2048]{1,0:T(8,128)(2,1)S(1)}, u32[]{:S(2)}) copy-start(bf16[256,2048]{1,0:T(8,128)(2,1)S(1)} %collective-permute-done.refs_0_) | copy-start | bytes 3145732
  67.9 1.8 %copy-start.2 = (bf16[256,2048]{1,0:T(8,128)(2,1)}, bf16[256,2048]{1,0:T(8,128)(2,1)S(1)}, u32[]{:S(2)}) copy-start(bf16[256,2048]{1,0:T(8,128)(2,1)S(1)} %collective-permute-done.1.refs_2_) | copy-start | bytes 3145732
  71.2 4.4 %collective-permute-start.2 = (bf16[2,256,2048]{2,1,0:T(8,128)(2,1)}, bf16[2,256,2048]{2,1,0:T(8,128)(2,1)S(1)}, u32[]{:S(2)}, u32[]{:S(2)}) collective-permute-start(bf16[2,256,2048]{2,1,0:T(8,128)(2,1)} %pad_maximum_fusion), channel_id=1, source_target_pairs={{0,1},{1,0},{2,3},{3,2},{4,5},{5,4},{6,7},{7,6},{8,9},{9,8},{10,11... | collective-permute-start | bytes 6291464 | tf_op jit(solution)/shard_map/ppermute | solution.py:113
  75.6 1.4 %copy-start = (bf16[2,256,2048]{2,1,0:T(8,128)(2,1)}, bf16[2,256,2048]{2,1,0:T(8,128)(2,1)S(1)}, u32[]{:S(2)}) copy-start(bf16[2,256,2048]{2,1,0:T(8,128)(2,1)S(1)} %collective-permute-done.2.refs_1_.refs_3_) | copy-start | bytes 6291460

commit v12 on v11

--- a/solution.py
+++ b/solution.py
@@ -64,7 +64,7 @@
 def convolve(rows, blocks, gate, skip, group_width):
     hops = len(blocks) - 1
     block_rows, channels = gate.shape
-    subs = next(n for n in (4, 2, 1) if channels % (n * LANES) == 0)
+    subs = next(n for n in (8, 4, 2, 1) if channels % (n * LANES) == 0)
     width = subs * LANES
     chunks = channels // width
     groups_per = width // group_width

time: 94.3 us -> 94.4 us (level)
  no operation moved by 1% of the time
where the time goes in v12:
time: 94.4 us; the launch traced here: 93.6 us
  waiting for transfers between devices  46.5 us (49%)
  blocking collectives  19.8 us (21%)
  Pallas kernels  16.7 us (18%)
  starting transfers between devices  3.84 us (4%)
  local copies, waits for them, and re-layouts  3.44 us (4%)
  other arithmetic  3.31 us (4%)
    ppermute x2, waiting for transfers between devices, from_behind(): return lax.ppermute(shard, axis, pairs)  44.2 us
    all_gather x1, blocking collectives, body(): all_taps = lax.all_gather(taps, 'seq', axis=0, tiled=True)  19.8 us
    pallas_call x1, Pallas kernels, convolve(): pl.pallas_call(kernel, grid=(chunks,), in_specs=[pl.BlockSpec((groups_per...  16.7 us
    ppermute x2, starting transfers between devices, from_behind(): return lax.ppermute(shard, axis, pairs)  3.83 us
    another operation x2, other arithmetic, body(): jnp.stack([jnp.where(first_core, signal, back_one), jnp.where(first_core,...  3.31 us
    ppermute x1, waiting for transfers between devices, body(): odd = lax.ppermute(outgoing, 'seq', swap)  2.26 us
  transfers between devices with their start and end apart: 3, of which 3 were waited for; matrix products, arithmetic and copies ran while one was open for 2% of the time, Pallas kernels for 0%

profile of v12, /device:TPU:8, one launch (start us, length us, event | category | flops | bytes accessed | tf_op | source)
XLA Modules:
  0.0 93.6 jit_solution(17821827283440053163)
XLA Ops:
  0.0 19.8 %all_gather.3 = bf16[1024,128]{1,0:T(8,128)(2,1)S(1)} all-gather(bf16[64,128]{1,0:T(8,128)(2,1)} %param.7), channel_id=1, replica_groups=mesh['rep'=2,'seq'=16] {'seq'}, dimensions={0}, use_global_device_ids=true | all-gather | bytes 278528 | tf_op jit(solution)/shard_map/all_gather | solution.py:98
  19.8 1.9 %collective-permute-start = (bf16[256,2048]{1,0:T(8,128)(2,1)}, bf16[256,2048]{1,0:T(8,128)(2,1)S(1)}, u32[]{:S(2)}, u32[]{:S(2)}) collective-permute-start(bf16[256,2048]{1,0:T(8,128)(2,1)} %refs_4_), channel_id=1, source_target_pairs={{0,4},{1,5},{2,6},{3,7},{4,8},{5,9},{6,10},{7,11},{8,12},{9,13},{1... | collective-permute-start | bytes 3145736 | tf_op jit(solution)/shard_map/ppermute | solution.py:17
  21.7 1.9 %collective-permute-start.1 = (bf16[256,2048]{1,0:T(8,128)(2,1)}, bf16[256,2048]{1,0:T(8,128)(2,1)S(1)}, u32[]{:S(2)}, u32[]{:S(2)}) collective-permute-start(bf16[256,2048]{1,0:T(8,128)(2,1)} %refs_4_), channel_id=1, source_target_pairs={{0,2},{1,3},{2,4},{3,5},{4,6},{5,7},{6,8},{7,9},{8,10},{9,11},{10,... | collective-permute-start | bytes 3145736 | tf_op jit(solution)/shard_map/ppermute | solution.py:17
  23.6 24.5 %collective-permute-done.refs_0_ = bf16[256,2048]{1,0:T(8,128)(2,1)S(1)} collective-permute-done((bf16[256,2048]{1,0:T(8,128)(2,1)}, bf16[256,2048]{1,0:T(8,128)(2,1)S(1)}, u32[]{:S(2)}, u32[]{:S(2)}) %collective-permute-start) | collective-permute-done | bytes 1048608 | tf_op jit(solution)/shard_map/ppermute | solution.py:17
  48.2 0.0 copy-start.1
  48.2 19.7 %collective-permute-done.1.refs_2_ = bf16[256,2048]{1,0:T(8,128)(2,1)S(1)} collective-permute-done((bf16[256,2048]{1,0:T(8,128)(2,1)}, bf16[256,2048]{1,0:T(8,128)(2,1)S(1)}, u32[]{:S(2)}, u32[]{:S(2)}) %collective-permute-start.1) | collective-permute-done | bytes 1048608 | tf_op jit(solution)/shard_map/ppermute | solution.py:17
  67.9 0.0 copy-start.2
  67.9 1.8 %select_bitcast_fusion.1 = (bf16[1,256,2048]{2,1,0:T(8,128)(2,1)S(1)}, bf16[1,256,2048]{2,1,0:T(8,128)(2,1)S(1)}) fusion(bf16[256,2048]{1,0:T(8,128)(2,1)} %refs_4_, bf16[256,2048]{1,0:T(8,128)(2,1)S(1)} %collective-permute-done.1.refs_2_, pred[]{:T(512)S(6)} %eq.5, bf16[256,2048]{1,0:T(8,128)(2,1)S(1)} %collective-permute-done.refs_0_), kind=kLoop, calls=%fused_computation.2 | loop fusion | flops 1048576 | bytes 5242881 | tf_op jit(solution)/shard_map/stack | solution.py:109
  69.6 0.0 copy-done.1
  69.7 0.0 copy-done.2
  69.7 1.5 %pad_maximum_fusion = bf16[2,256,2048]{2,1,0:T(8,128)(2,1)} fusion(bf16[1,256,2048]{2,1,0:T(8,128)(2,1)S(1)} %get-tuple-element.10, bf16[1,256,2048]{2,1,0:T(8,128)(2,1)S(1)} %get-tuple-element.9), kind=kLoop, calls=%fused_computation | loop fusion | flops 1048576 | bytes 4194304 | tf_op jit(solution)/shard_map/stack | solution.py:109
  71.2 0.0 collective-permute-start.2
  71.2 0.1 copy.6
  71.4 0.8 rev.3
  72.2 1.1 %concatenate.3.rows_ref = f32[128,1280]{1,0:T(8,128)} concatenate(f32[128,129]{1,0:T(8,128)S(1)} %broadcast_in_dim.6, bf16[128,1024]{1,0:T(8,128)(2,1)S(1)} %rev.3, f32[128,127]{1,0:T(8,128)S(1)} %broadcast_in_dim.7), dimensions={1} | concatenate | bytes 1048576 | tf_op jit(solution)/shard_map/concatenate | solution.py:25
  73.3 2.3 %collective-permute-done.2.refs_1_.refs_3_ = bf16[2,256,2048]{2,1,0:T(8,128)(2,1)S(1)} collective-permute-done((bf16[2,256,2048]{2,1,0:T(8,128)(2,1)}, bf16[2,256,2048]{2,1,0:T(8,128)(2,1)S(1)}, u32[]{:S(2)}, u32[]{:S(2)}) %collective-permute-start.2) | collective-permute-done | bytes 2097184 | tf_op jit(solution)/shard_map/ppermute | solution.py:113
  75.6 0.0 copy-start
  75.6 1.4 %copy-done = bf16[2,256,2048]{2,1,0:T(8,128)(2,1)} copy-done((bf16[2,256,2048]{2,1,0:T(8,128)(2,1)}, bf16[2,256,2048]{2,1,0:T(8,128)(2,1)S(1)}, u32[]{:S(2)}) %copy-start) | copy-done | bytes 2097176
  76.9 16.7 %shard_map.46 = bf16[256,2048]{1,0:T(8,128)(2,1)} custom-call(f32[128,1280]{1,0:T(8,128)} %concatenate.3.rows_ref, bf16[256,2048]{1,0:T(8,128)(2,1)} %copy-done.1, bf16[2,256,2048]{2,1,0:T(8,128)(2,1)} %copy-done, bf16[256,2048]{1,0:T(8,128)(2,1)} %copy-done.2, bf16[2,256,2048]{2,1,0:T(8,128)(2,1)} %copy-done, bf16[256,2048]{1,0:T(8,128)(2,1)} %refs_4_, ...), custom_call_target="tpu_custom_call" | custom-call | tf_op jit(solution)/shard_map/pallas_call | solution.py:82
  (2 shorter events, 0.0 us)
Async XLA Ops:
  19.8 28.4 %collective-permute-start = (bf16[256,2048]{1,0:T(8,128)(2,1)}, bf16[256,2048]{1,0:T(8,128)(2,1)S(1)}, u32[]{:S(2)}, u32[]{:S(2)}) collective-permute-start(bf16[256,2048]{1,0:T(8,128)(2,1)} %refs_4_), channel_id=1, source_target_pairs={{0,4},{1,5},{2,6},{3,7},{4,8},{5,9},{6,10},{7,11},{8,12},{9,13},{1... | collective-permute-start | bytes 3145736 | tf_op jit(solution)/shard_map/ppermute | solution.py:17
  21.7 46.2 %collective-permute-start.1 = (bf16[256,2048]{1,0:T(8,128)(2,1)}, bf16[256,2048]{1,0:T(8,128)(2,1)S(1)}, u32[]{:S(2)}, u32[]{:S(2)}) collective-permute-start(bf16[256,2048]{1,0:T(8,128)(2,1)} %refs_4_), channel_id=1, source_target_pairs={{0,2},{1,3},{2,4},{3,5},{4,6},{5,7},{6,8},{7,9},{8,10},{9,11},{10,... | collective-permute-start | bytes 3145736 | tf_op jit(solution)/shard_map/ppermute | solution.py:17
  48.2 21.5 %copy-start.1 = (bf16[256,2048]{1,0:T(8,128)(2,1)}, bf16[256,2048]{1,0:T(8,128)(2,1)S(1)}, u32[]{:S(2)}) copy-start(bf16[256,2048]{1,0:T(8,128)(2,1)S(1)} %collective-permute-done.refs_0_) | copy-start | bytes 3145732
  67.9 1.8 %copy-start.2 = (bf16[256,2048]{1,0:T(8,128)(2,1)}, bf16[256,2048]{1,0:T(8,128)(2,1)S(1)}, u32[]{:S(2)}) copy-start(bf16[256,2048]{1,0:T(8,128)(2,1)S(1)} %collective-permute-done.1.refs_2_) | copy-start | bytes 3145732
  71.2 4.4 %collective-permute-start.2 = (bf16[2,256,2048]{2,1,0:T(8,128)(2,1)}, bf16[2,256,2048]{2,1,0:T(8,128)(2,1)S(1)}, u32[]{:S(2)}, u32[]{:S(2)}) collective-permute-start(bf16[2,256,2048]{2,1,0:T(8,128)(2,1)} %pad_maximum_fusion), channel_id=1, source_target_pairs={{0,1},{1,0},{2,3},{3,2},{4,5},{5,4},{6,7},{7,6},{8,9},{9,8},{10,11... | collective-permute-start | bytes 6291464 | tf_op jit(solution)/shard_map/ppermute | solution.py:113
  75.6 1.4 %copy-start = (bf16[2,256,2048]{2,1,0:T(8,128)(2,1)}, bf16[2,256,2048]{2,1,0:T(8,128)(2,1)S(1)}, u32[]{:S(2)}) copy-start(bf16[2,256,2048]{2,1,0:T(8,128)(2,1)S(1)} %collective-permute-done.2.refs_1_.refs_3_) | copy-start | bytes 6291460
